TPU v7x, 128 devices: a whole 4x4x4 slice. The times are simulated.
128 devices in a mesh: group: 8 (over z, core), member: 16 (over y, x).
Axes of the slice: x: 4, y: 4, z: 4, core: 2. Of those that a mesh axis runs over, the one named last changes fastest.
Arguments:
- embeddings: bfloat16 [65536, 1024], P(('group', 'member')), may hold values from -70 to 70
- coarse_ids: int32 [65536, 1], P(('group', 'member')), may hold values from 0 to 127; in each aligned block of 512 rows (0 to 511, 512 to 1023, ...) at most 8 rows name the same one
- centroid_seeds: bfloat16 [4096, 1024], P('group'), may hold values from -1 to 1
Outputs:
- refined_centroids: float32 [4096, 1024], P(('group', 'member'))
- row_energy: float32 [65536], P(('group', 'member'))
Inputs may be any that keep to these rules, and one draw needn't show every extreme that they name: `coarse_ids`: in the rows of one device no coarse cluster is named by more than 8 rows.
All inputs are finite; a program needn't handle non-finite values.
Results may differ from a plain program's by a relative error of at most 0.00092.
Values may be sent and summed in bfloat16 or wider, within the bound.
No kernel may reach another device: no remote copies, remote signals or barrier semaphores. Data moves between devices by JAX's collectives and lax.ppermute only.
A program may use at most 64 MiB of HBM per device.

v0:
```python
import math

import jax
import jax.numpy as jnp
from jax import lax
from jax.sharding import Mesh
from jax.sharding import PartitionSpec as P


K = 512
ITERS = 2


smoothing_scale = 0.004
prior_mass = 32.0
empty_mark = 2.0


ALL = ("z", "core", "yhi", "ylo", "x")
ROUTE = ("z", "yhi", "core", "ylo", "x")
TEAM = ("core", "ylo", "x")
PLANE = ("ylo", "x")


def steps(embeddings, coarse_ids, centroid_seeds):
    rows_dev, features = embeddings.shape
    cores = lax.axis_size("core")
    plane = lax.axis_size("ylo") * lax.axis_size("x")
    members = cores * plane
    clusters = members * lax.axis_size("z") * lax.axis_size("yhi")
    capacity = 2 * rows_dev // clusters
    share_rows = K // members
    core = lax.axis_index("core")
    yhi = lax.axis_index("yhi")
    spot = lax.axis_index(PLANE)
    first_row = lax.axis_index(TEAM) * share_rows
    partner = lax.ppermute(centroid_seeds, "core", [(0, 1), (1, 0)])
    seeds16 = jnp.where(core == yhi, centroid_seeds, partner)
    widened = embeddings.astype(jnp.float32)
    unit_rows = (
        widened
        * lax.rsqrt(jnp.mean(widened * widened, axis=1, keepdims=True) + 1e-06)
        / math.sqrt(features)
    ).astype(jnp.bfloat16)
    cluster_of = coarse_ids[:, 0]
    onehot = (cluster_of[:, None] == jnp.arange(clusters, dtype=jnp.int32)[None, :]).astype(
        jnp.int32
    )
    row_rank = jnp.sum((jnp.cumsum(onehot, axis=0) - onehot) * onehot, axis=1)
    slot_of = cluster_of * capacity + row_rank
    placement = (
        slot_of[None, :] == jnp.arange(clusters * capacity, dtype=jnp.int32)[:, None]
    ).astype(jnp.bfloat16)
    filled = jnp.sum(placement.astype(jnp.float32), axis=1) > 0.5
    empty_row = jnp.where(
        jnp.arange(features) == 0, jnp.bfloat16(empty_mark), jnp.bfloat16(0)
    ).astype(jnp.bfloat16)
    gathered = jnp.dot(placement, unit_rows, preferred_element_type=jnp.float32).astype(
        jnp.bfloat16
    )
    packed = jnp.where(filled[:, None], gathered, empty_row[None, :])
    arrived = lax.all_to_all(packed, ROUTE, split_axis=0, concat_axis=0, tiled=True)
    slot_mask = (arrived[:, 0].astype(jnp.float32) < 1.5).astype(jnp.float32)
    seeds = seeds16.astype(jnp.float32)
    own = lax.dynamic_slice_in_dim(seeds, first_row, share_rows, 0)
    prototype_lowbits = seeds16
    half_quadratic_length = 0.5 * jnp.sum(seeds * seeds, axis=1)
    for iteration in range(ITERS):
        similarity_logits = (
            jnp.dot(arrived, prototype_lowbits.T, preferred_element_type=jnp.float32)
            - half_quadratic_length[None, :]
        ) / smoothing_scale
        row_max = jnp.max(similarity_logits, axis=1, keepdims=True)
        powers = jnp.exp(similarity_logits - row_max)
        row_sum = jnp.sum(powers, axis=1, keepdims=True)
        weights = (powers / row_sum * slot_mask[:, None]).astype(jnp.bfloat16)
        closing_log_partition = row_max[:, 0] + jnp.log(row_sum[:, 0])
        if iteration + 1 == ITERS:
            returned = lax.all_to_all(
                smoothing_scale * closing_log_partition, ROUTE, split_axis=0, concat_axis=0,
                tiled=True,
            )
        weighted = jnp.einsum("rk,rd->kd", weights, arrived, preferred_element_type=jnp.float32)
        masses = jnp.sum(weights.astype(jnp.float32), axis=0)
        combined = jnp.concatenate(
            [
                weighted.reshape(members, share_rows * features),
                jnp.pad(masses.reshape(members, share_rows), ((0, 0), (0, 128 - share_rows))),
            ],
            axis=1,
        )
        width = combined.shape[1]
        by_core = combined.reshape(cores, plane, width)
        mine = lax.dynamic_index_in_dim(by_core, core, 0, keepdims=False)
        theirs = lax.dynamic_index_in_dim(by_core, 1 - core, 0, keepdims=False)
        halves = mine + lax.ppermute(theirs, "core", [(0, 1), (1, 0)])
        reduced = lax.dynamic_index_in_dim(halves, spot, 0, keepdims=True)
        for shift in range(1, plane):
            outgoing = lax.dynamic_index_in_dim(halves, (spot + shift) % plane, 0, keepdims=True)
            incoming = lax.ppermute(
                outgoing, PLANE, [(i, (i + shift) % plane) for i in range(plane)]
            )
            reduced = reduced + incoming
        weighted_own = reduced[0, : share_rows * features].reshape(share_rows, features)
        masses_own = reduced[0, share_rows * features : share_rows * features + share_rows]
        own = (weighted_own + prior_mass * own) / (masses_own + prior_mass)[:, None]
        if iteration + 1 < ITERS:
            half_own = 0.5 * jnp.sum(own * own, axis=1)
            high = lax.reduce_precision(half_own, exponent_bits=8, mantissa_bits=7)
            rest = half_own - high
            middle = lax.reduce_precision(rest, exponent_bits=8, mantissa_bits=7)
            low = rest - middle
            block = jnp.concatenate(
                [
                    own.astype(jnp.bfloat16),
                    jnp.stack([high, middle, low], axis=1).astype(jnp.bfloat16),
                    jnp.zeros((share_rows, 125), jnp.bfloat16),
                ],
                axis=1,
            )
            by_shift = jnp.stack(
                [block]
                + [
                    lax.ppermute(block, PLANE, [(i, (i + shift) % plane) for i in range(plane)])
                    for shift in range(1, plane)
                ]
            )
            on_plane = jnp.take(by_shift, (spot - jnp.arange(plane)) % plane, axis=0)
            partner_plane = lax.ppermute(on_plane, "core", [(0, 1), (1, 0)])
            everyone = jnp.concatenate(
                [
                    jnp.where(core == 0, on_plane, partner_plane),
                    jnp.where(core == 0, partner_plane, on_plane),
                ],
                axis=0,
            ).reshape(K, features + 128)
            prototype_lowbits = everyone[:, :features]
            parts = everyone[:, features : features + 3].astype(jnp.float32)
            half_quadratic_length = (parts[:, 0] + parts[:, 1]) + parts[:, 2]
    own_slot = slot_of[None, :] == jnp.arange(clusters * capacity, dtype=jnp.int32)[:, None]
    row_energy = jnp.sum(jnp.where(own_slot, returned[:, None], 0.0), axis=0)
    refined = lax.ppermute(own, ("core", "yhi"), [(0, 0), (1, 2), (2, 1), (3, 3)])
    return (refined, row_energy)


def solution(mesh):
    groups, members = mesh.devices.shape
    fine = Mesh(mesh.devices.reshape(groups // 2, 2, 2, members // 8, 4), ALL)
    in_specs = (P(ALL, None), P(ALL, None), P(("z", "core"), None))
    out_specs = (P(ALL, None), P(ALL))
    return jax.shard_map(steps, mesh=fine, in_specs=in_specs, out_specs=out_specs, check_vma=False)
```

profile of v0, /device:TPU:1, one launch (start us, length us, event | category | flops | bytes accessed | tf_op | source)
XLA Modules:
  0.0 151.6 jit_solution(14811632398694739680)
XLA Ops:
  0.7 0.9 copy.29
  1.8 0.9 fusion.26
  2.8 0.7 multiply_add_fusion
  4.1 2.7 %select_bitcast_fusion = bf16[128,8,1024]{2,1,0:T(8,128)(2,1)} fusion(pred[1024]{0:T(1024)(128)(4,1)S(1)} %broadcast_compare_fusion, bf16[512,1024]{1,0:T(8,128)(2,1)S(1)} %copy-done.2, bf16[1024]{0:T(1024)(128)(2,1)S(1)} %fusion.30, f32[512]{0:T(512)S(1)} %add_rsqrt_fusion, s32[512]{0:T(512)S(1)} %multiply_add_fusion), kind=kOutput, calls=%fused_computation.20 | convolution fusion | flops 1078460416 | bytes 3152896 | tf_op jit(solution)/shard_map/dot_general | solution.py:58
  6.8 11.5 %all-to-all-start = ((bf16[128,8,1024]{2,1,0:T(8,128)(2,1)}), bf16[128,8,1024]{2,1,0:T(8,128)(2,1)S(1)}, u32[]{:S(2)}, u32[]{:S(2)}) async-start(bf16[128,8,1024]{2,1,0:T(8,128)(2,1)} %select_bitcast_fusion), calls=%async_computation | async-start | bytes 4194304 | tf_op jit(solution)/shard_map/all_to_all | solution.py:62
  18.3 1.1 collective-permute-start
  19.4 2.4 %collective-permute-done = bf16[512,1024]{1,0:T(8,128)(2,1)} collective-permute-done((bf16[512,1024]{1,0:T(8,128)(2,1)S(1)}, bf16[512,1024]{1,0:T(8,128)(2,1)}, u32[]{:S(2)}, u32[]{:S(2)}) %collective-permute-start) | collective-permute-done | bytes 1048608 | tf_op jit(solution)/shard_map/ppermute | solution.py:37
  21.9 2.8 %fusion.45 = (f32[512,1024]{1,0:T(8,128)}, bf16[512,1024]{1,0:T(8,128)(2,1)S(1)}) fusion(bf16[512,1024]{1,0:T(8,128)(2,1)} %param.5, bf16[512,1024]{1,0:T(8,128)(2,1)} %collective-permute-done, pred[]{:T(512)S(6)} %eq.90), kind=kLoop, calls=%fused_computation.135 | loop fusion | flops 1048576 | bytes 5242881 | tf_op jit(solution)/shard_map/convert_element_type | solution.py:64
  24.9 23.7 %all-to-all-done = bf16[128,8,1024]{2,1,0:T(8,128)(2,1)S(1)} async-done(((bf16[128,8,1024]{2,1,0:T(8,128)(2,1)}), bf16[128,8,1024]{2,1,0:T(8,128)(2,1)S(1)}, u32[]{:S(2)}, u32[]{:S(2)}) %all-to-all-start) | async-done | bytes 2097184 | tf_op jit(solution)/shard_map/all_to_all | solution.py:62
  48.7 1.3 fusion.5
  50.5 0.8 convert_reduce_fusion.1
  51.3 2.6 %fusion.40 = f32[512,1024]{1,0:T(8,128)} fusion(bf16[1024,512]{0,1:T(8,128)(2,1)S(1)} %get-tuple-element.9, bf16[128,8,1024]{2,1,0:T(8,128)(2,1)S(1)} %all-to-all-done), kind=kOutput, calls=%fused_computation.130 | convolution fusion | flops 1073741824 | bytes 5242880 | tf_op jit(solution)/shard_map/rk,rd->kd/dot_general | solution.py:83
  53.9 1.7 %concatenate.23 = f32[2,8,32768]{2,1,0:T(8,128)S(1)} reshape(f32[512,1024]{1,0:T(8,128)} %fusion.40) | data formatting | bytes 4194304 | tf_op jit(solution)/shard_map/concatenate | solution.py:85
  55.9 1.3 collective-permute-start.1
  57.2 2.4 %collective-permute-done.1 = f32[8,32896]{1,0:T(8,128)} collective-permute-done((f32[8,32896]{1,0:T(8,128)S(1)}, f32[8,32896]{1,0:T(8,128)}, u32[]{:S(2)}, u32[]{:S(2)}) %collective-permute-start.1) | collective-permute-done | bytes 1052704 | tf_op jit(solution)/shard_map/ppermute | solution.py:96
  59.6 1.3 fusion.18
  61.0 0.6 constant_dynamic-slice_fusion.12
  62.0 1.3 collective-permute-start.3
  63.3 0.7 collective-permute-start.4
  64.0 1.7 %collective-permute-start.5 = (f32[1,32896]{1,0:T(1,128)S(1)}, f32[1,32896]{1,0:T(1,128)S(1)}, u32[]{:S(2)}, u32[]{:S(2)}) collective-permute-start(f32[1,32896]{1,0:T(1,128)S(1)} %get-tuple-element.23), channel_id=1, source_target_pairs={{0,4},{1,5},{2,6},{3,7},{4,0},{5,1},{6,2},{7,3},{8,12},{9,13},{10,... | collective-permute-start | bytes 394760 | tf_op jit(solution)/shard_map/ppermute | solution.py:100
  66.1 6.7 %collective-permute-done.2 = f32[1,32896]{1,0:T(1,128)S(1)} collective-permute-done((f32[1,32896]{1,0:T(1,128)S(1)}, f32[1,32896]{1,0:T(1,128)S(1)}, u32[]{:S(2)}, u32[]{:S(2)}) %collective-permute-start.2) | collective-permute-done | bytes 131616 | tf_op jit(solution)/shard_map/ppermute | solution.py:100
  73.2 4.5 %collective-permute-done.5 = f32[1,32896]{1,0:T(1,128)S(1)} collective-permute-done((f32[1,32896]{1,0:T(1,128)S(1)}, f32[1,32896]{1,0:T(1,128)S(1)}, u32[]{:S(2)}, u32[]{:S(2)}) %collective-permute-start.5) | collective-permute-done | bytes 131616 | tf_op jit(solution)/shard_map/ppermute | solution.py:100
  79.0 1.1 multiply_reduce_fusion.1
  80.9 2.9 %collective-permute-start.10 = (bf16[32,1152]{1,0:T(8,128)(2,1)S(1)}, bf16[32,1152]{1,0:T(8,128)(2,1)S(1)}, u32[]{:S(2)}, u32[]{:S(2)}) collective-permute-start(bf16[32,1152]{1,0:T(8,128)(2,1)S(1)} %concatenate.26), channel_id=1, source_target_pairs={{0,2},{1,3},{2,4},{3,5},{4,6},{5,7},{6,0},{7,1},{8,10},{9,11},{10,... | collective-permute-start | bytes 221192 | tf_op jit(solution)/shard_map/ppermute | solution.py:124
  83.7 0.7 collective-permute-start.11
  84.4 2.2 %collective-permute-start.12 = (bf16[32,1152]{1,0:T(8,128)(2,1)S(1)}, bf16[32,1152]{1,0:T(8,128)(2,1)S(1)}, u32[]{:S(2)}, u32[]{:S(2)}) collective-permute-start(bf16[32,1152]{1,0:T(8,128)(2,1)S(1)} %concatenate.26), channel_id=1, source_target_pairs={{0,4},{1,5},{2,6},{3,7},{4,0},{5,1},{6,2},{7,3},{8,12},{9,13},{10,... | collective-permute-start | bytes 221192 | tf_op jit(solution)/shard_map/ppermute | solution.py:124
  86.7 2.0 %collective-permute-start.14 = (bf16[32,1152]{1,0:T(8,128)(2,1)S(1)}, bf16[32,1152]{1,0:T(8,128)(2,1)S(1)}, u32[]{:S(2)}, u32[]{:S(2)}) collective-permute-start(bf16[32,1152]{1,0:T(8,128)(2,1)S(1)} %concatenate.26), channel_id=1, source_target_pairs={{0,6},{1,7},{2,0},{3,1},{4,2},{5,3},{6,4},{7,5},{8,14},{9,15},{10,... | collective-permute-start | bytes 221192 | tf_op jit(solution)/shard_map/ppermute | solution.py:124
  88.7 1.2 collective-permute-start.15
  90.0 1.9 %collective-permute-done.13 = bf16[32,1152]{1,0:T(8,128)(2,1)S(1)} collective-permute-done((bf16[32,1152]{1,0:T(8,128)(2,1)S(1)}, bf16[32,1152]{1,0:T(8,128)(2,1)S(1)}, u32[]{:S(2)}, u32[]{:S(2)}) %collective-permute-start.13) | collective-permute-done | bytes 73760 | tf_op jit(solution)/shard_map/ppermute | solution.py:124
  93.3 5.1 %collective-permute-start.16 = (bf16[8,32,1152]{2,1,0:T(8,128)(2,1)S(1)}, bf16[8,32,1152]{2,1,0:T(8,128)(2,1)}, u32[]{:S(2)}, u32[]{:S(2)}) collective-permute-start(bf16[8,32,1152]{2,1,0:T(8,128)(2,1)S(1)} %broadcast_select_fusion.1), channel_id=1, source_target_pairs={{0,16},{16,0},{1,17},{17,1},{2,18},{18,2},{3,19},{19,3},{4,20},{20... | collective-permute-start | bytes 1769480 | tf_op jit(solution)/shard_map/ppermute | solution.py:129
  98.4 1.8 %collective-permute-done.16 = bf16[8,32,1152]{2,1,0:T(8,128)(2,1)} collective-permute-done((bf16[8,32,1152]{2,1,0:T(8,128)(2,1)S(1)}, bf16[8,32,1152]{2,1,0:T(8,128)(2,1)}, u32[]{:S(2)}, u32[]{:S(2)}) %collective-permute-start.16) | collective-permute-done | bytes 589856 | tf_op jit(solution)/shard_map/ppermute | solution.py:129
  100.2 1.3 broadcast_select_fusion.3
  101.7 1.3 fusion.6
  103.5 0.8 convert_reduce_fusion
  104.3 2.6 %fusion.37 = f32[512,1024]{1,0:T(8,128)} fusion(bf16[1024,512]{0,1:T(8,128)(2,1)S(1)} %get-tuple-element.3, bf16[128,8,1024]{2,1,0:T(8,128)(2,1)S(1)} %copy-done.1), kind=kOutput, calls=%fused_computation.127 | convolution fusion | flops 1073741824 | bytes 5242880 | tf_op jit(solution)/shard_map/rk,rd->kd/dot_general | solution.py:83
  107.0 1.7 %concatenate.28 = f32[2,8,32768]{2,1,0:T(8,128)S(1)} reshape(f32[512,1024]{1,0:T(8,128)} %fusion.37) | data formatting | bytes 4194304 | tf_op jit(solution)/shard_map/concatenate | solution.py:85
  109.3 2.3 %collective-permute-done.17 = f32[8,32896]{1,0:T(8,128)S(1)} collective-permute-done((f32[8,32896]{1,0:T(8,128)S(1)}, f32[8,32896]{1,0:T(8,128)S(1)}, u32[]{:S(2)}, u32[]{:S(2)}) %collective-permute-start.17) | collective-permute-done | bytes 1052704 | tf_op jit(solution)/shard_map/ppermute | solution.py:96
  112.4 1.3 collective-permute-start.18
  113.7 4.0 %collective-permute-start.19 = (f32[1,32896]{1,0:T(1,128)S(1)}, f32[1,32896]{1,0:T(1,128)S(1)}, u32[]{:S(2)}, u32[]{:S(2)}) collective-permute-start(f32[1,32896]{1,0:T(1,128)S(1)} %get-tuple-element.18), channel_id=1, source_target_pairs={{0,2},{1,3},{2,4},{3,5},{4,6},{5,7},{6,0},{7,1},{8,10},{9,11},{10,... | collective-permute-start | bytes 394760 | tf_op jit(solution)/shard_map/ppermute | solution.py:100
  117.8 2.3 %collective-permute-start.22 = (f32[1,32896]{1,0:T(1,128)S(1)}, f32[1,32896]{1,0:T(1,128)S(1)}, u32[]{:S(2)}, u32[]{:S(2)}) collective-permute-start(f32[1,32896]{1,0:T(1,128)S(1)} %get-tuple-element.15), channel_id=1, source_target_pairs={{0,5},{1,6},{2,7},{3,0},{4,1},{5,2},{6,3},{7,4},{8,13},{9,14},{10,... | collective-permute-start | bytes 394760 | tf_op jit(solution)/shard_map/ppermute | solution.py:100
  120.1 1.2 collective-permute-start.23
  121.2 2.9 %collective-permute-done.19 = f32[1,32896]{1,0:T(1,128)S(1)} collective-permute-done((f32[1,32896]{1,0:T(1,128)S(1)}, f32[1,32896]{1,0:T(1,128)S(1)}, u32[]{:S(2)}, u32[]{:S(2)}) %collective-permute-start.19) | collective-permute-done | bytes 131616 | tf_op jit(solution)/shard_map/ppermute | solution.py:100
  124.3 16.4 %all_to_all.18 = f32[128,8,1]{1,2,0:T(1,128)S(1)} all-to-all(f32[128,8,1]{1,2,0:T(1,128)S(1)} %bitcast.87), channel_id=1, replica_groups=mesh['z'=4,'core'=2,'yhi'=2,'ylo'=2,'x'=4] {'z','yhi','core','ylo','x'}, dimensions={0} | all-to-all | bytes 8192 | tf_op jit(solution)/shard_map/all_to_all | solution.py:79
  141.2 0.8 reduce.13
  143.1 3.2 %collective-permute-start.25 = (f32[32,1024]{1,0:T(8,128)S(1)}, f32[32,1024]{1,0:T(8,128)S(1)}, u32[]{:S(2)}, u32[]{:S(2)}) collective-permute-start(f32[32,1024]{1,0:T(8,128)S(1)} %add_divide_fusion), channel_id=1, source_target_pairs={{0,0},{8,16},{16,8},{24,24},{1,1},{9,17},{17,9},{25,25},{2,2},{10,... | collective-permute-start | bytes 393224 | tf_op jit(solution)/shard_map/ppermute | solution.py:142
  146.3 0.9 select_reduce_fusion
  147.3 3.7 %collective-permute-done.25 = f32[32,1024]{1,0:T(8,128)S(1)} collective-permute-done((f32[32,1024]{1,0:T(8,128)S(1)}, f32[32,1024]{1,0:T(8,128)S(1)}, u32[]{:S(2)}, u32[]{:S(2)}) %collective-permute-start.25) | collective-permute-done | bytes 131104 | tf_op jit(solution)/shard_map/ppermute | solution.py:142
  150.9 0.7 copy.45
  (98 shorter events, 10.6 us)
Async XLA Ops:
  0.6 3.1 %copy-start.2 = (bf16[512,1024]{1,0:T(8,128)(2,1)S(1)}, bf16[512,1024]{1,0:T(8,128)(2,1)}, u32[]{:S(2)}) copy-start(bf16[512,1024]{1,0:T(8,128)(2,1)} %param.3) | copy-start | bytes 3145732
  6.8 11.5 %copy-start.3 = (bf16[512,1024]{1,0:T(8,128)(2,1)S(1)}, bf16[512,1024]{1,0:T(8,128)(2,1)}, u32[]{:S(2)}) copy-start(bf16[512,1024]{1,0:T(8,128)(2,1)} %param.5) | copy-start | bytes 3145732
  6.8 41.8 %all-to-all-start = ((bf16[128,8,1024]{2,1,0:T(8,128)(2,1)}), bf16[128,8,1024]{2,1,0:T(8,128)(2,1)S(1)}, u32[]{:S(2)}, u32[]{:S(2)}) async-start(bf16[128,8,1024]{2,1,0:T(8,128)(2,1)} %select_bitcast_fusion), calls=%async_computation | async-start | bytes 4194304 | tf_op jit(solution)/shard_map/all_to_all | solution.py:62
  18.3 3.6 %collective-permute-start = (bf16[512,1024]{1,0:T(8,128)(2,1)S(1)}, bf16[512,1024]{1,0:T(8,128)(2,1)}, u32[]{:S(2)}, u32[]{:S(2)}) collective-permute-start(bf16[512,1024]{1,0:T(8,128)(2,1)S(1)} %copy-done.3), channel_id=1, source_target_pairs={{0,16},{16,0},{1,17},{17,1},{2,18},{18,2},{3,19},{19,3},{4,20},{20... | collective-permute-start | bytes 3145736 | tf_op jit(solution)/shard_map/ppermute | solution.py:37
  48.6 2.8 %copy-start = (bf16[128,8,1024]{2,1,0:T(8,128)(2,1)}, bf16[128,8,1024]{2,1,0:T(8,128)(2,1)S(1)}, u32[]{:S(2)}) copy-start(bf16[128,8,1024]{2,1,0:T(8,128)(2,1)S(1)} %all-to-all-done) | copy-start | bytes 6291460
  55.9 3.8 %collective-permute-start.1 = (f32[8,32896]{1,0:T(8,128)S(1)}, f32[8,32896]{1,0:T(8,128)}, u32[]{:S(2)}, u32[]{:S(2)}) collective-permute-start(f32[8,32896]{1,0:T(8,128)S(1)} %fusion.15), channel_id=1, source_target_pairs={{0,16},{16,0},{1,17},{17,1},{2,18},{18,2},{3,19},{19,3},{4,20},{20... | collective-permute-start | bytes 3158024 | tf_op jit(solution)/shard_map/ppermute | solution.py:96
  61.6 11.2 %collective-permute-start.2 = (f32[1,32896]{1,0:T(1,128)S(1)}, f32[1,32896]{1,0:T(1,128)S(1)}, u32[]{:S(2)}, u32[]{:S(2)}) collective-permute-start(f32[1,32896]{1,0:T(1,128)S(1)} %get-tuple-element.19), channel_id=1, source_target_pairs={{0,1},{1,2},{2,3},{3,4},{4,5},{5,6},{6,7},{7,0},{8,9},{9,10},{10,1... | collective-permute-start | bytes 394760 | tf_op jit(solution)/shard_map/ppermute | solution.py:100
  62.0 10.8 %collective-permute-start.3 = (f32[1,32896]{1,0:T(1,128)S(1)}, f32[1,32896]{1,0:T(1,128)S(1)}, u32[]{:S(2)}, u32[]{:S(2)}) collective-permute-start(f32[1,32896]{1,0:T(1,128)S(1)} %get-tuple-element.25), channel_id=1, source_target_pairs={{0,2},{1,3},{2,4},{3,5},{4,6},{5,7},{6,0},{7,1},{8,10},{9,11},{10,... | collective-permute-start | bytes 394760 | tf_op jit(solution)/shard_map/ppermute | solution.py:100
  63.3 9.9 %collective-permute-start.4 = (f32[1,32896]{1,0:T(1,128)S(1)}, f32[1,32896]{1,0:T(1,128)S(1)}, u32[]{:S(2)}, u32[]{:S(2)}) collective-permute-start(f32[1,32896]{1,0:T(1,128)S(1)} %get-tuple-element.24), channel_id=1, source_target_pairs={{0,3},{1,4},{2,5},{3,6},{4,7},{5,0},{6,1},{7,2},{8,11},{9,12},{10,... | collective-permute-start | bytes 394760 | tf_op jit(solution)/shard_map/ppermute | solution.py:100
  64.0 13.7 %collective-permute-start.5 = (f32[1,32896]{1,0:T(1,128)S(1)}, f32[1,32896]{1,0:T(1,128)S(1)}, u32[]{:S(2)}, u32[]{:S(2)}) collective-permute-start(f32[1,32896]{1,0:T(1,128)S(1)} %get-tuple-element.23), channel_id=1, source_target_pairs={{0,4},{1,5},{2,6},{3,7},{4,0},{5,1},{6,2},{7,3},{8,12},{9,13},{10,... | collective-permute-start | bytes 394760 | tf_op jit(solution)/shard_map/ppermute | solution.py:100
  65.7 12.0 %collective-permute-start.6 = (f32[1,32896]{1,0:T(1,128)S(1)}, f32[1,32896]{1,0:T(1,128)S(1)}, u32[]{:S(2)}, u32[]{:S(2)}) collective-permute-start(f32[1,32896]{1,0:T(1,128)S(1)} %get-tuple-element.22), channel_id=1, source_target_pairs={{0,5},{1,6},{2,7},{3,0},{4,1},{5,2},{6,3},{7,4},{8,13},{9,14},{10,... | collective-permute-start | bytes 394760 | tf_op jit(solution)/shard_map/ppermute | solution.py:100
  72.8 5.3 %collective-permute-start.7 = (f32[1,32896]{1,0:T(1,128)S(1)}, f32[1,32896]{1,0:T(1,128)S(1)}, u32[]{:S(2)}, u32[]{:S(2)}) collective-permute-start(f32[1,32896]{1,0:T(1,128)S(1)} %get-tuple-element.21), channel_id=1, source_target_pairs={{0,6},{1,7},{2,0},{3,1},{4,2},{5,3},{6,4},{7,5},{8,14},{9,15},{10,... | collective-permute-start | bytes 394760 | tf_op jit(solution)/shard_map/ppermute | solution.py:100
  72.8 5.3 %collective-permute-start.8 = (f32[1,32896]{1,0:T(1,128)S(1)}, f32[1,32896]{1,0:T(1,128)S(1)}, u32[]{:S(2)}, u32[]{:S(2)}) collective-permute-start(f32[1,32896]{1,0:T(1,128)S(1)} %get-tuple-element.20), channel_id=1, source_target_pairs={{0,7},{1,0},{2,1},{3,2},{4,3},{5,4},{6,5},{7,6},{8,15},{9,8},{10,9... | collective-permute-start | bytes 394760 | tf_op jit(solution)/shard_map/ppermute | solution.py:100
  80.5 6.2 %collective-permute-start.9 = (bf16[32,1152]{1,0:T(8,128)(2,1)S(1)}, bf16[32,1152]{1,0:T(8,128)(2,1)S(1)}, u32[]{:S(2)}, u32[]{:S(2)}) collective-permute-start(bf16[32,1152]{1,0:T(8,128)(2,1)S(1)} %concatenate.26), channel_id=1, source_target_pairs={{0,1},{1,2},{2,3},{3,4},{4,5},{5,6},{6,7},{7,0},{8,9},{9,10},{10,1... | collective-permute-start | bytes 221192 | tf_op jit(solution)/shard_map/ppermute | solution.py:124
  80.9 7.8 %collective-permute-start.10 = (bf16[32,1152]{1,0:T(8,128)(2,1)S(1)}, bf16[32,1152]{1,0:T(8,128)(2,1)S(1)}, u32[]{:S(2)}, u32[]{:S(2)}) collective-permute-start(bf16[32,1152]{1,0:T(8,128)(2,1)S(1)} %concatenate.26), channel_id=1, source_target_pairs={{0,2},{1,3},{2,4},{3,5},{4,6},{5,7},{6,0},{7,1},{8,10},{9,11},{10,... | collective-permute-start | bytes 221192 | tf_op jit(solution)/shard_map/ppermute | solution.py:124
  83.7 6.2 %collective-permute-start.11 = (bf16[32,1152]{1,0:T(8,128)(2,1)S(1)}, bf16[32,1152]{1,0:T(8,128)(2,1)S(1)}, u32[]{:S(2)}, u32[]{:S(2)}) collective-permute-start(bf16[32,1152]{1,0:T(8,128)(2,1)S(1)} %concatenate.26), channel_id=1, source_target_pairs={{0,3},{1,4},{2,5},{3,6},{4,7},{5,0},{6,1},{7,2},{8,11},{9,12},{10,... | collective-permute-start | bytes 221192 | tf_op jit(solution)/shard_map/ppermute | solution.py:124
  84.4 5.6 %collective-permute-start.12 = (bf16[32,1152]{1,0:T(8,128)(2,1)S(1)}, bf16[32,1152]{1,0:T(8,128)(2,1)S(1)}, u32[]{:S(2)}, u32[]{:S(2)}) collective-permute-start(bf16[32,1152]{1,0:T(8,128)(2,1)S(1)} %concatenate.26), channel_id=1, source_target_pairs={{0,4},{1,5},{2,6},{3,7},{4,0},{5,1},{6,2},{7,3},{8,12},{9,13},{10,... | collective-permute-start | bytes 221192 | tf_op jit(solution)/shard_map/ppermute | solution.py:124
  86.6 5.3 %collective-permute-start.13 = (bf16[32,1152]{1,0:T(8,128)(2,1)S(1)}, bf16[32,1152]{1,0:T(8,128)(2,1)S(1)}, u32[]{:S(2)}, u32[]{:S(2)}) collective-permute-start(bf16[32,1152]{1,0:T(8,128)(2,1)S(1)} %concatenate.26), channel_id=1, source_target_pairs={{0,5},{1,6},{2,7},{3,0},{4,1},{5,2},{6,3},{7,4},{8,13},{9,14},{10,... | collective-permute-start | bytes 221192 | tf_op jit(solution)/shard_map/ppermute | solution.py:124
  86.7 5.2 %collective-permute-start.14 = (bf16[32,1152]{1,0:T(8,128)(2,1)S(1)}, bf16[32,1152]{1,0:T(8,128)(2,1)S(1)}, u32[]{:S(2)}, u32[]{:S(2)}) collective-permute-start(bf16[32,1152]{1,0:T(8,128)(2,1)S(1)} %concatenate.26), channel_id=1, source_target_pairs={{0,6},{1,7},{2,0},{3,1},{4,2},{5,3},{6,4},{7,5},{8,14},{9,15},{10,... | collective-permute-start | bytes 221192 | tf_op jit(solution)/shard_map/ppermute | solution.py:124
  88.7 3.8 %collective-permute-start.15 = (bf16[32,1152]{1,0:T(8,128)(2,1)S(1)}, bf16[32,1152]{1,0:T(8,128)(2,1)S(1)}, u32[]{:S(2)}, u32[]{:S(2)}) collective-permute-start(bf16[32,1152]{1,0:T(8,128)(2,1)S(1)} %concatenate.26), channel_id=1, source_target_pairs={{0,7},{1,0},{2,1},{3,2},{4,3},{5,4},{6,5},{7,6},{8,15},{9,8},{10,9... | collective-permute-start | bytes 221192 | tf_op jit(solution)/shard_map/ppermute | solution.py:124
  93.3 6.9 %collective-permute-start.16 = (bf16[8,32,1152]{2,1,0:T(8,128)(2,1)S(1)}, bf16[8,32,1152]{2,1,0:T(8,128)(2,1)}, u32[]{:S(2)}, u32[]{:S(2)}) collective-permute-start(bf16[8,32,1152]{2,1,0:T(8,128)(2,1)S(1)} %broadcast_select_fusion.1), channel_id=1, source_target_pairs={{0,16},{16,0},{1,17},{17,1},{2,18},{18,2},{3,19},{19,3},{4,20},{20... | collective-permute-start | bytes 1769480 | tf_op jit(solution)/shard_map/ppermute | solution.py:129
  98.4 3.3 %copy-start.1 = (bf16[128,8,1024]{2,1,0:T(8,128)(2,1)S(1)}, bf16[128,8,1024]{2,1,0:T(8,128)(2,1)}, u32[]{:S(2)}) copy-start(bf16[128,8,1024]{2,1,0:T(8,128)(2,1)} %copy-done) | copy-start | bytes 6291460
  108.9 2.7 %collective-permute-start.17 = (f32[8,32896]{1,0:T(8,128)S(1)}, f32[8,32896]{1,0:T(8,128)S(1)}, u32[]{:S(2)}, u32[]{:S(2)}) collective-permute-start(f32[8,32896]{1,0:T(8,128)S(1)} %fusion.10), channel_id=1, source_target_pairs={{0,16},{16,0},{1,17},{17,1},{2,18},{18,2},{3,19},{19,3},{4,20},{20... | collective-permute-start | bytes 3158024 | tf_op jit(solution)/shard_map/ppermute | solution.py:96
  112.4 7.7 %collective-permute-start.18 = (f32[1,32896]{1,0:T(1,128)S(1)}, f32[1,32896]{1,0:T(1,128)S(1)}, u32[]{:S(2)}, u32[]{:S(2)}) collective-permute-start(f32[1,32896]{1,0:T(1,128)S(1)} %get-tuple-element.12), channel_id=1, source_target_pairs={{0,1},{1,2},{2,3},{3,4},{4,5},{5,6},{6,7},{7,0},{8,9},{9,10},{10,1... | collective-permute-start | bytes 394760 | tf_op jit(solution)/shard_map/ppermute | solution.py:100
  113.7 10.5 %collective-permute-start.19 = (f32[1,32896]{1,0:T(1,128)S(1)}, f32[1,32896]{1,0:T(1,128)S(1)}, u32[]{:S(2)}, u32[]{:S(2)}) collective-permute-start(f32[1,32896]{1,0:T(1,128)S(1)} %get-tuple-element.18), channel_id=1, source_target_pairs={{0,2},{1,3},{2,4},{3,5},{4,6},{5,7},{6,0},{7,1},{8,10},{9,11},{10,... | collective-permute-start | bytes 394760 | tf_op jit(solution)/shard_map/ppermute | solution.py:100
  117.7 24.4 %collective-permute-start.20 = (f32[1,32896]{1,0:T(1,128)S(1)}, f32[1,32896]{1,0:T(1,128)S(1)}, u32[]{:S(2)}, u32[]{:S(2)}) collective-permute-start(f32[1,32896]{1,0:T(1,128)S(1)} %get-tuple-element.17), channel_id=1, source_target_pairs={{0,3},{1,4},{2,5},{3,6},{4,7},{5,0},{6,1},{7,2},{8,11},{9,12},{10,... | collective-permute-start | bytes 394760 | tf_op jit(solution)/shard_map/ppermute | solution.py:100
  117.7 24.5 %collective-permute-start.21 = (f32[1,32896]{1,0:T(1,128)S(1)}, f32[1,32896]{1,0:T(1,128)S(1)}, u32[]{:S(2)}, u32[]{:S(2)}) collective-permute-start(f32[1,32896]{1,0:T(1,128)S(1)} %get-tuple-element.16), channel_id=1, source_target_pairs={{0,4},{1,5},{2,6},{3,7},{4,0},{5,1},{6,2},{7,3},{8,12},{9,13},{10,... | collective-permute-start | bytes 394760 | tf_op jit(solution)/shard_map/ppermute | solution.py:100
  117.8 24.4 %collective-permute-start.22 = (f32[1,32896]{1,0:T(1,128)S(1)}, f32[1,32896]{1,0:T(1,128)S(1)}, u32[]{:S(2)}, u32[]{:S(2)}) collective-permute-start(f32[1,32896]{1,0:T(1,128)S(1)} %get-tuple-element.15), channel_id=1, source_target_pairs={{0,5},{1,6},{2,7},{3,0},{4,1},{5,2},{6,3},{7,4},{8,13},{9,14},{10,... | collective-permute-start | bytes 394760 | tf_op jit(solution)/shard_map/ppermute | solution.py:100
  120.1 22.1 %collective-permute-start.23 = (f32[1,32896]{1,0:T(1,128)S(1)}, f32[1,32896]{1,0:T(1,128)S(1)}, u32[]{:S(2)}, u32[]{:S(2)}) collective-permute-start(f32[1,32896]{1,0:T(1,128)S(1)} %get-tuple-element.14), channel_id=1, source_target_pairs={{0,6},{1,7},{2,0},{3,1},{4,2},{5,3},{6,4},{7,5},{8,14},{9,15},{10,... | collective-permute-start | bytes 394760 | tf_op jit(solution)/shard_map/ppermute | solution.py:100
  124.2 18.0 %collective-permute-start.24 = (f32[1,32896]{1,0:T(1,128)S(1)}, f32[1,32896]{1,0:T(1,128)S(1)}, u32[]{:S(2)}, u32[]{:S(2)}) collective-permute-start(f32[1,32896]{1,0:T(1,128)S(1)} %get-tuple-element.13), channel_id=1, source_target_pairs={{0,7},{1,0},{2,1},{3,2},{4,3},{5,4},{6,5},{7,6},{8,15},{9,8},{10,9... | collective-permute-start | bytes 394760 | tf_op jit(solution)/shard_map/ppermute | solution.py:100
  143.1 7.8 %collective-permute-start.25 = (f32[32,1024]{1,0:T(8,128)S(1)}, f32[32,1024]{1,0:T(8,128)S(1)}, u32[]{:S(2)}, u32[]{:S(2)}) collective-permute-start(f32[32,1024]{1,0:T(8,128)S(1)} %add_divide_fusion), channel_id=1, source_target_pairs={{0,0},{8,16},{16,8},{24,24},{1,1},{9,17},{17,9},{25,25},{2,2},{10,... | collective-permute-start | bytes 393224 | tf_op jit(solution)/shard_map/ppermute | solution.py:142
where the time goes:
time: 152 us
  waiting for transfers between devices  53.7 us (35%)
  starting transfers between devices  45.4 us (30%)
  blocking collectives  16.4 us (11%)
  other arithmetic  15.3 us (10%)
  matrix products  10.5 us (7%)
  local copies, waits for them, and re-layouts  9.2 us (6%)
    all_to_all x1, waiting for transfers between devices, steps(): lax.all_to_all(packed, ROUTE, split_axis=0, concat_axis=0, tiled=True)  23.7 us
    all_to_all x1, blocking collectives, steps(): lax.all_to_all(smoothing_scale * closing_log_partition, ROUTE, split_axis...  16.4 us
    ppermute x14, waiting for transfers between devices, steps(): lax.ppermute(outgoing, PLANE, [(i, (i + shift) % plane) for i in range(pl...  14.9 us
    ppermute x14, starting transfers between devices, steps(): lax.ppermute(outgoing, PLANE, [(i, (i + shift) % plane) for i in range(pl...  13.3 us
    all_to_all x1, starting transfers between devices, steps(): lax.all_to_all(packed, ROUTE, split_axis=0, concat_axis=0, tiled=True)  11.5 us
    ppermute x7, starting transfers between devices, steps(): lax.ppermute(block, PLANE, [(i, (i + shift) % plane) for i in range(plane)])  9.28 us
    dot_general x2, matrix products, steps(): jnp.einsum('rk,rd->kd', weights, arrived, preferred_element_type=jnp.floa...  5.22 us
    ppermute x1, starting transfers between devices, steps(): partner_plane = lax.ppermute(on_plane, 'core', [(0, 1), (1, 0)])  5.1 us
  transfers between devices with their start and end apart: 27, of which 14 were waited for; matrix products, arithmetic and copies ran while one was open for 4% of the time, Pallas kernels for 0%

commit v1 on v0

--- a/solution.py
+++ b/solution.py
@@ -80,20 +80,24 @@
                 smoothing_scale * closing_log_partition, ROUTE, split_axis=0, concat_axis=0,
                 tiled=True,
             )
-        weighted = jnp.einsum("rk,rd->kd", weights, arrived, preferred_element_type=jnp.float32)
-        masses = jnp.sum(weights.astype(jnp.float32), axis=0)
-        combined = jnp.concatenate(
-            [
-                weighted.reshape(members, share_rows * features),
-                jnp.pad(masses.reshape(members, share_rows), ((0, 0), (0, 128 - share_rows))),
-            ],
-            axis=1,
-        )
-        width = combined.shape[1]
-        by_core = combined.reshape(cores, plane, width)
-        mine = lax.dynamic_index_in_dim(by_core, core, 0, keepdims=False)
-        theirs = lax.dynamic_index_in_dim(by_core, 1 - core, 0, keepdims=False)
-        halves = mine + lax.ppermute(theirs, "core", [(0, 1), (1, 0)])
+        half_rows = K // cores
+
+        def block_sums(side):
+            picked = lax.dynamic_slice_in_dim(weights, side * half_rows, half_rows, 1)
+            weighted = jnp.einsum(
+                "rk,rd->kd", picked, arrived, preferred_element_type=jnp.float32
+            )
+            masses = jnp.sum(picked.astype(jnp.float32), axis=0)
+            return jnp.concatenate(
+                [
+                    weighted.reshape(plane, share_rows * features),
+                    jnp.pad(masses.reshape(plane, share_rows), ((0, 0), (0, 128 - share_rows))),
+                ],
+                axis=1,
+            )
+
+        incoming = lax.ppermute(block_sums(1 - core), "core", [(0, 1), (1, 0)])
+        halves = block_sums(core) + incoming
         reduced = lax.dynamic_index_in_dim(halves, spot, 0, keepdims=True)
         for shift in range(1, plane):
             outgoing = lax.dynamic_index_in_dim(halves, (spot + shift) % plane, 0, keepdims=True)

time: 152 us -> 164 us (1.079)
  other arithmetic: 15.3 us -> 25.6 us
  waiting for transfers between devices: 53.7 us -> 46.1 us
  local copies, waits for them, and re-layouts: 9.2 us -> 15.9 us
  matrix products: 10.5 us -> 12.4 us
    reshape x2 -> x8, local copies, waits for them, and re-layouts: 0.15 us -> 8.94 us  [the longest x4 8.64 us: block_sums(): weighted.reshape(plane, share_rows * features)]
    ppermute x2, waiting for transfers between devices: 4.72 us -> 0.01 us  [steps(): incoming = lax.ppermute(block_sums(1 - core), 'core', [(0, 1), (1, 0)])]
    concatenate x0 -> x2, other arithmetic: none -> 4.58 us  [block_sums(): jnp.concatenate([weighted.reshape(plane, share_rows * features), jnp.pad(...]
    concatenate x4 -> x0, local copies, waits for them, and re-layouts: 3.51 us -> none  [steps(): jnp.concatenate([weighted.reshape(members, share_rows * features), jnp.pa...]
    ppermute x14, waiting for transfers between devices: 14.9 us -> 12.7 us  [steps(): lax.ppermute(outgoing, PLANE, [(i, (i + shift) % plane) for i in range(pl...]
    dot_general x2 -> x4, matrix products: 5.22 us -> 6.92 us  [block_sums(): jnp.einsum('rk,rd->kd', picked, arrived, preferred_element_type=jnp.float32)]
    convert_element_type x0 -> x2, other arithmetic: none -> 1.65 us  [steps(): weights = (powers / row_sum * slot_mask[:, None]).astype(jnp.bfloat16)]
  transfers between devices with their start and end apart: 27 -> 27, of which waited for: 14 -> 9; matrix products, arithmetic and copies ran while one was open for 4% -> 9% of each run, Pallas kernels for 0% -> 0%
where the time goes in v1:
time: 164 us; the launch traced here: 163 us
  waiting for transfers between devices  46.1 us (28%)
  starting transfers between devices  45.3 us (28%)
  other arithmetic  25.6 us (16%)
  blocking collectives  17.1 us (10%)
  local copies, waits for them, and re-layouts  15.9 us (10%)
  matrix products  12.4 us (8%)
    all_to_all x1, waiting for transfers between devices, steps(): lax.all_to_all(packed, ROUTE, split_axis=0, concat_axis=0, tiled=True)  23.7 us
    all_to_all x1, blocking collectives, steps(): lax.all_to_all(smoothing_scale * closing_log_partition, ROUTE, split_axis...  17.1 us
    ppermute x14, starting transfers between devices, steps(): lax.ppermute(outgoing, PLANE, [(i, (i + shift) % plane) for i in range(pl...  13.6 us
    ppermute x14, waiting for transfers between devices, steps(): lax.ppermute(outgoing, PLANE, [(i, (i + shift) % plane) for i in range(pl...  12.7 us
    all_to_all x1, starting transfers between devices, steps(): lax.all_to_all(packed, ROUTE, split_axis=0, concat_axis=0, tiled=True)  11.5 us
    ppermute x7, starting transfers between devices, steps(): lax.ppermute(block, PLANE, [(i, (i + shift) % plane) for i in range(plane)])  10.1 us
    reshape x4, local copies, waits for them, and re-layouts, block_sums(): weighted.reshape(plane, share_rows * features)  8.64 us
    dot_general x4, matrix products, block_sums(): jnp.einsum('rk,rd->kd', picked, arrived, preferred_element_type=jnp.float32)  6.92 us
  transfers between devices with their start and end apart: 27, of which 9 were waited for; matrix products, arithmetic and copies ran while one was open for 9% of the time, Pallas kernels for 0%

profile of v1, /device:TPU:1, one launch (start us, length us, event | category | flops | bytes accessed | tf_op | source)
XLA Modules:
  0.0 163.4 jit_solution(5779898471268521333)
XLA Ops:
  0.7 0.9 copy.29
  1.8 0.9 fusion.26
  4.1 2.7 %select_bitcast_fusion = bf16[128,8,1024]{2,1,0:T(8,128)(2,1)} fusion(pred[1024]{0:T(1024)(128)(4,1)S(1)} %broadcast_compare_fusion, bf16[512,1024]{1,0:T(8,128)(2,1)S(1)} %copy-done, bf16[1024]{0:T(1024)(128)(2,1)S(1)} %fusion.34, f32[512]{0:T(512)S(1)} %add_rsqrt_fusion, s32[512]{0:T(512)S(1)} %multiply_add_fusion), kind=kOutput, calls=%fused_computation.14 | convolution fusion | flops 1078460416 | bytes 3152896 | tf_op jit(solution)/shard_map/dot_general | solution.py:58
  6.8 11.5 %all-to-all-start = ((bf16[128,8,1024]{2,1,0:T(8,128)(2,1)}), bf16[128,8,1024]{2,1,0:T(8,128)(2,1)S(1)}, u32[]{:S(2)}, u32[]{:S(2)}) async-start(bf16[128,8,1024]{2,1,0:T(8,128)(2,1)} %select_bitcast_fusion), calls=%async_computation | async-start | bytes 4194304 | tf_op jit(solution)/shard_map/all_to_all | solution.py:62
  18.3 1.1 collective-permute-start
  19.4 2.4 %collective-permute-done = bf16[512,1024]{1,0:T(8,128)(2,1)} collective-permute-done((bf16[512,1024]{1,0:T(8,128)(2,1)S(1)}, bf16[512,1024]{1,0:T(8,128)(2,1)}, u32[]{:S(2)}, u32[]{:S(2)}) %collective-permute-start) | collective-permute-done | bytes 1048608 | tf_op jit(solution)/shard_map/ppermute | solution.py:37
  21.9 2.8 %fusion.49 = (f32[512,1024]{1,0:T(8,128)}, bf16[512,1024]{1,0:T(8,128)(2,1)S(1)}) fusion(bf16[512,1024]{1,0:T(8,128)(2,1)} %param.5, bf16[512,1024]{1,0:T(8,128)(2,1)} %collective-permute-done, pred[]{:T(512)S(6)} %eq.90), kind=kLoop, calls=%fused_computation.136 | loop fusion | flops 1048576 | bytes 5242881 | tf_op jit(solution)/shard_map/convert_element_type | solution.py:64
  24.9 23.7 %all-to-all-done = bf16[128,8,1024]{2,1,0:T(8,128)(2,1)S(1)} async-done(((bf16[128,8,1024]{2,1,0:T(8,128)(2,1)}), bf16[128,8,1024]{2,1,0:T(8,128)(2,1)S(1)}, u32[]{:S(2)}, u32[]{:S(2)}) %all-to-all-start) | async-done | bytes 2097184 | tf_op jit(solution)/shard_map/all_to_all | solution.py:62
  48.7 1.4 fusion.5
  51.9 1.7 %fusion.21 = f32[256,1024]{1,0:T(8,128)} fusion(bf16[1024,512]{1,0:T(8,128)(2,1)S(1)} %multiply_convert_fusion.1, s32[]{:T(128)S(6)} %select_n.170, bf16[128,8,1024]{2,1,0:T(8,128)(2,1)S(1)} %all-to-all-done), kind=kOutput, calls=%fused_computation.50 | convolution fusion | flops 536870912 | bytes 3670020 | tf_op jit(solution)/shard_map/rk,rd->kd/dot_general | solution.py:87
  53.6 2.4 %reshape.227 = f32[8,32768]{1,0:T(8,128)} reshape(f32[256,1024]{1,0:T(8,128)} %fusion.21) | data formatting | bytes 2097152 | tf_op jit(solution)/shard_map/reshape | solution.py:93
  56.0 2.3 %select_maximum_fusion.2 = f32[8,32896]{1,0:T(8,128)} fusion(f32[8,32]{1,0:T(8,128)S(1)} %reshape.228, f32[8,32768]{1,0:T(8,128)} %reshape.227), kind=kLoop, calls=%fused_computation.27 | loop fusion | flops 789504 | bytes 2102272 | tf_op jit(solution)/shard_map/concatenate | solution.py:91
  58.3 1.3 collective-permute-start.1
  59.6 1.7 %fusion.23 = f32[256,1024]{1,0:T(8,128)} fusion(bf16[1024,512]{1,0:T(8,128)(2,1)S(1)} %multiply_convert_fusion.1, s32[]{:T(128)S(6)} %select_n.169, bf16[128,8,1024]{2,1,0:T(8,128)(2,1)S(1)} %all-to-all-done), kind=kOutput, calls=%fused_computation.52 | convolution fusion | flops 536870912 | bytes 3670020 | tf_op jit(solution)/shard_map/rk,rd->kd/dot_general | solution.py:87
  61.4 2.4 %reshape.225 = f32[8,32768]{1,0:T(8,128)} reshape(f32[256,1024]{1,0:T(8,128)} %fusion.23) | data formatting | bytes 2097152 | tf_op jit(solution)/shard_map/reshape | solution.py:93
  63.8 1.6 %fusion.10 = f32[8,32896]{1,0:T(8,128)S(1)} fusion(f32[8,32896]{1,0:T(8,128)} %collective-permute-done.1, f32[8,32]{1,0:T(8,128)S(1)} %reshape.226, f32[8,32768]{1,0:T(8,128)} %reshape.225), kind=kLoop, calls=%fused_computation.29 | loop fusion | flops 1052672 | bytes 3154944 | tf_op jit(solution)/shard_map/add | solution.py:100
  65.4 1.4 constant_dynamic-slice_fusion.13
  67.1 1.3 collective-permute-start.3
  69.6 1.7 %collective-permute-start.5 = (f32[1,32896]{1,0:T(1,128)}, f32[1,32896]{1,0:T(1,128)}, u32[]{:S(2)}, u32[]{:S(2)}) collective-permute-start(f32[1,32896]{1,0:T(1,128)} %get-tuple-element.23), channel_id=1, source_target_pairs={{0,4},{1,5},{2,6},{3,7},{4,0},{5,1},{6,2},{7,3},{8,12},{9,13},{10,... | collective-permute-start | bytes 394760 | tf_op jit(solution)/shard_map/ppermute | solution.py:104
  71.7 6.4 %collective-permute-done.2 = f32[1,32896]{1,0:T(1,128)S(1)} collective-permute-done((f32[1,32896]{1,0:T(1,128)S(1)}, f32[1,32896]{1,0:T(1,128)S(1)}, u32[]{:S(2)}, u32[]{:S(2)}) %collective-permute-start.2) | collective-permute-done | bytes 131616 | tf_op jit(solution)/shard_map/ppermute | solution.py:104
  79.4 1.3 pad_clamp_fusion
  80.7 2.2 %collective-permute-done.5 = f32[1,32896]{1,0:T(1,128)} collective-permute-done((f32[1,32896]{1,0:T(1,128)}, f32[1,32896]{1,0:T(1,128)}, u32[]{:S(2)}, u32[]{:S(2)}) %collective-permute-start.5) | collective-permute-done | bytes 131616 | tf_op jit(solution)/shard_map/ppermute | solution.py:104
  83.6 1.7 %add_add_fusion.1 = f32[1,32896]{1,0:T(1,128)S(1)} fusion(f32[1,32896]{1,0:T(1,128)} %collective-permute-done.8, f32[1,32896]{1,0:T(1,128)} %collective-permute-done.7, f32[1,32896]{1,0:T(1,128)} %collective-permute-done.6, f32[1,32896]{1,0:T(1,128)} %collective-permute-done.5, f32[1,32896]{1,0:T(1,128)} %collective-permute-done.4, f32[1,32896]{1,0:T(1,128)} %copy-done.3, ...), kind=kLoop, calls=%fused_computation.62 | loop fusion | flops 230272 | bytes 1184260 | tf_op jit(solution)/shard_map/add | solution.py:107
  85.6 1.1 multiply_reduce_fusion.1
  87.3 3.8 %collective-permute-start.10 = (bf16[32,1152]{1,0:T(8,128)(2,1)S(1)}, bf16[32,1152]{1,0:T(8,128)(2,1)S(1)}, u32[]{:S(2)}, u32[]{:S(2)}) collective-permute-start(bf16[32,1152]{1,0:T(8,128)(2,1)S(1)} %concatenate.21), channel_id=1, source_target_pairs={{0,2},{1,3},{2,4},{3,5},{4,6},{5,7},{6,0},{7,1},{8,10},{9,11},{10,... | collective-permute-start | bytes 221192 | tf_op jit(solution)/shard_map/ppermute | solution.py:128
  91.7 2.2 %collective-permute-start.12 = (bf16[32,1152]{1,0:T(8,128)(2,1)S(1)}, bf16[32,1152]{1,0:T(8,128)(2,1)S(1)}, u32[]{:S(2)}, u32[]{:S(2)}) collective-permute-start(bf16[32,1152]{1,0:T(8,128)(2,1)S(1)} %concatenate.21), channel_id=1, source_target_pairs={{0,4},{1,5},{2,6},{3,7},{4,0},{5,1},{6,2},{7,3},{8,12},{9,13},{10,... | collective-permute-start | bytes 221192 | tf_op jit(solution)/shard_map/ppermute | solution.py:128
  94.4 1.6 collective-permute-start.14
  96.0 1.4 collective-permute-start.15
  97.4 1.9 %collective-permute-done.12 = bf16[32,1152]{1,0:T(8,128)(2,1)S(1)} collective-permute-done((bf16[32,1152]{1,0:T(8,128)(2,1)S(1)}, bf16[32,1152]{1,0:T(8,128)(2,1)S(1)}, u32[]{:S(2)}, u32[]{:S(2)}) %collective-permute-start.12) | collective-permute-done | bytes 73760 | tf_op jit(solution)/shard_map/ppermute | solution.py:128
  100.3 4.1 %collective-permute-start.16 = (bf16[8,32,1152]{2,1,0:T(8,128)(2,1)S(1)}, bf16[8,32,1152]{2,1,0:T(8,128)(2,1)}, u32[]{:S(2)}, u32[]{:S(2)}) collective-permute-start(bf16[8,32,1152]{2,1,0:T(8,128)(2,1)S(1)} %broadcast_select_fusion.1), channel_id=1, source_target_pairs={{0,16},{16,0},{1,17},{17,1},{2,18},{18,2},{3,19},{19,3},{4,20},{20... | collective-permute-start | bytes 1769480 | tf_op jit(solution)/shard_map/ppermute | solution.py:133
  104.4 1.8 %collective-permute-done.16 = bf16[8,32,1152]{2,1,0:T(8,128)(2,1)} collective-permute-done((bf16[8,32,1152]{2,1,0:T(8,128)(2,1)S(1)}, bf16[8,32,1152]{2,1,0:T(8,128)(2,1)}, u32[]{:S(2)}, u32[]{:S(2)}) %collective-permute-start.16) | collective-permute-done | bytes 589856 | tf_op jit(solution)/shard_map/ppermute | solution.py:133
  106.2 1.3 broadcast_select_fusion.3
  107.7 1.4 fusion.6
  110.8 1.7 %fusion.17 = f32[256,1024]{1,0:T(8,128)} fusion(bf16[1024,512]{1,0:T(8,128)(2,1)S(1)} %multiply_convert_fusion, s32[]{:T(128)S(6)} %select_n.170, bf16[128,8,1024]{2,1,0:T(8,128)(2,1)S(1)} %all-to-all-done), kind=kOutput, calls=%fused_computation.46 | convolution fusion | flops 536870912 | bytes 3670020 | tf_op jit(solution)/shard_map/rk,rd->kd/dot_general | solution.py:87
  112.5 2.4 %reshape.232 = f32[8,32768]{1,0:T(8,128)} reshape(f32[256,1024]{1,0:T(8,128)} %fusion.17) | data formatting | bytes 2097152 | tf_op jit(solution)/shard_map/reshape | solution.py:93
  115.0 2.3 %select_maximum_fusion = f32[8,32896]{1,0:T(8,128)} fusion(f32[8,32]{1,0:T(8,128)S(1)} %reshape.233, f32[8,32768]{1,0:T(8,128)} %reshape.232), kind=kLoop, calls=%fused_computation.24 | loop fusion | flops 789504 | bytes 2102272 | tf_op jit(solution)/shard_map/concatenate | solution.py:91
  117.7 1.7 %fusion.19 = f32[256,1024]{1,0:T(8,128)} fusion(bf16[1024,512]{1,0:T(8,128)(2,1)S(1)} %multiply_convert_fusion, s32[]{:T(128)S(6)} %select_n.169, bf16[128,8,1024]{2,1,0:T(8,128)(2,1)S(1)} %all-to-all-done), kind=kOutput, calls=%fused_computation.48 | convolution fusion | flops 536870912 | bytes 3670020 | tf_op jit(solution)/shard_map/rk,rd->kd/dot_general | solution.py:87
  119.4 1.4 reshape.230
  120.9 1.3 fusion.9
  122.9 1.5 collective-permute-start.18
  124.4 4.0 %collective-permute-start.19 = (f32[1,32896]{1,0:T(1,128)S(1)}, f32[1,32896]{1,0:T(1,128)S(1)}, u32[]{:S(2)}, u32[]{:S(2)}) collective-permute-start(f32[1,32896]{1,0:T(1,128)S(1)} %get-tuple-element.18), channel_id=1, source_target_pairs={{0,2},{1,3},{2,4},{3,5},{4,6},{5,7},{6,0},{7,1},{8,10},{9,11},{10,... | collective-permute-start | bytes 394760 | tf_op jit(solution)/shard_map/ppermute | solution.py:104
  128.5 2.3 %collective-permute-start.22 = (f32[1,32896]{1,0:T(1,128)S(1)}, f32[1,32896]{1,0:T(1,128)S(1)}, u32[]{:S(2)}, u32[]{:S(2)}) collective-permute-start(f32[1,32896]{1,0:T(1,128)S(1)} %get-tuple-element.15), channel_id=1, source_target_pairs={{0,5},{1,6},{2,7},{3,0},{4,1},{5,2},{6,3},{7,4},{8,13},{9,14},{10,... | collective-permute-start | bytes 394760 | tf_op jit(solution)/shard_map/ppermute | solution.py:104
  130.8 1.2 collective-permute-start.23
  132.0 3.4 %collective-permute-done.19 = f32[1,32896]{1,0:T(1,128)S(1)} collective-permute-done((f32[1,32896]{1,0:T(1,128)S(1)}, f32[1,32896]{1,0:T(1,128)S(1)}, u32[]{:S(2)}, u32[]{:S(2)}) %collective-permute-start.19) | collective-permute-done | bytes 131616 | tf_op jit(solution)/shard_map/ppermute | solution.py:104
  135.5 17.1 %all_to_all.18 = f32[128,8,1]{1,2,0:T(1,128)S(1)} all-to-all(f32[128,8,1]{1,2,0:T(1,128)S(1)} %bitcast.73), channel_id=1, replica_groups=mesh['z'=4,'core'=2,'yhi'=2,'ylo'=2,'x'=4] {'z','yhi','core','ylo','x'}, dimensions={0} | all-to-all | bytes 8192 | tf_op jit(solution)/shard_map/all_to_all | solution.py:79
  154.9 3.2 %collective-permute-start.25 = (f32[32,1024]{1,0:T(8,128)S(1)}, f32[32,1024]{1,0:T(8,128)S(1)}, u32[]{:S(2)}, u32[]{:S(2)}) collective-permute-start(f32[32,1024]{1,0:T(8,128)S(1)} %add_divide_fusion), channel_id=1, source_target_pairs={{0,0},{8,16},{16,8},{24,24},{1,1},{9,17},{17,9},{25,25},{2,2},{10,... | collective-permute-start | bytes 393224 | tf_op jit(solution)/shard_map/ppermute | solution.py:146
  158.2 0.9 select_reduce_fusion
  159.1 3.6 %collective-permute-done.25 = f32[32,1024]{1,0:T(8,128)S(1)} collective-permute-done((f32[32,1024]{1,0:T(8,128)S(1)}, f32[32,1024]{1,0:T(8,128)S(1)}, u32[]{:S(2)}, u32[]{:S(2)}) %collective-permute-start.25) | collective-permute-done | bytes 131104 | tf_op jit(solution)/shard_map/ppermute | solution.py:146
  (114 shorter events, 17.1 us)
Async XLA Ops:
  0.6 3.1 %copy-start = (bf16[512,1024]{1,0:T(8,128)(2,1)S(1)}, bf16[512,1024]{1,0:T(8,128)(2,1)}, u32[]{:S(2)}) copy-start(bf16[512,1024]{1,0:T(8,128)(2,1)} %param.3) | copy-start | bytes 3145732
  3.4 3.3 %copy-start.6 = (s32[512]{0:T(512)}, s32[512]{0:T(512)S(1)}, u32[]{:S(2)}) copy-start(s32[512]{0:T(512)S(1)} %multiply_add_fusion) | copy-start | bytes 6148
  6.8 11.5 %copy-start.1 = (bf16[512,1024]{1,0:T(8,128)(2,1)S(1)}, bf16[512,1024]{1,0:T(8,128)(2,1)}, u32[]{:S(2)}) copy-start(bf16[512,1024]{1,0:T(8,128)(2,1)} %param.5) | copy-start | bytes 3145732
  6.8 41.8 %all-to-all-start = ((bf16[128,8,1024]{2,1,0:T(8,128)(2,1)}), bf16[128,8,1024]{2,1,0:T(8,128)(2,1)S(1)}, u32[]{:S(2)}, u32[]{:S(2)}) async-start(bf16[128,8,1024]{2,1,0:T(8,128)(2,1)} %select_bitcast_fusion), calls=%async_computation | async-start | bytes 4194304 | tf_op jit(solution)/shard_map/all_to_all | solution.py:62
  18.3 3.6 %collective-permute-start = (bf16[512,1024]{1,0:T(8,128)(2,1)S(1)}, bf16[512,1024]{1,0:T(8,128)(2,1)}, u32[]{:S(2)}, u32[]{:S(2)}) collective-permute-start(bf16[512,1024]{1,0:T(8,128)(2,1)S(1)} %copy-done.1), channel_id=1, source_target_pairs={{0,16},{16,0},{1,17},{17,1},{2,18},{18,2},{3,19},{19,3},{4,20},{20... | collective-permute-start | bytes 3145736 | tf_op jit(solution)/shard_map/ppermute | solution.py:37
  48.7 2.0 %copy-start.4 = (f32[1024]{0:T(1024)}, f32[1024]{0:T(1024)S(1)}, u32[]{:S(2)}) copy-start(f32[1024]{0:T(1024)S(1)} %convert_reduce_fusion.5) | copy-start | bytes 12292
  58.3 5.5 %collective-permute-start.1 = (f32[8,32896]{1,0:T(8,128)}, f32[8,32896]{1,0:T(8,128)}, u32[]{:S(2)}, u32[]{:S(2)}) collective-permute-start(f32[8,32896]{1,0:T(8,128)} %select_maximum_fusion.2), channel_id=1, source_target_pairs={{0,16},{16,0},{1,17},{17,1},{2,18},{18,2},{3,19},{19,3},{4,20},{20... | collective-permute-start | bytes 3158024 | tf_op jit(solution)/shard_map/ppermute | solution.py:99
  66.8 11.3 %collective-permute-start.2 = (f32[1,32896]{1,0:T(1,128)S(1)}, f32[1,32896]{1,0:T(1,128)S(1)}, u32[]{:S(2)}, u32[]{:S(2)}) collective-permute-start(f32[1,32896]{1,0:T(1,128)S(1)} %get-tuple-element.19), channel_id=1, source_target_pairs={{0,1},{1,2},{2,3},{3,4},{4,5},{5,6},{6,7},{7,0},{8,9},{9,10},{10,1... | collective-permute-start | bytes 394760 | tf_op jit(solution)/shard_map/ppermute | solution.py:104
  67.1 11.0 %collective-permute-start.3 = (f32[1,32896]{1,0:T(1,128)S(1)}, f32[1,32896]{1,0:T(1,128)S(1)}, u32[]{:S(2)}, u32[]{:S(2)}) collective-permute-start(f32[1,32896]{1,0:T(1,128)S(1)} %get-tuple-element.25), channel_id=1, source_target_pairs={{0,2},{1,3},{2,4},{3,5},{4,6},{5,7},{6,0},{7,1},{8,10},{9,11},{10,... | collective-permute-start | bytes 394760 | tf_op jit(solution)/shard_map/ppermute | solution.py:104
  69.0 11.7 %collective-permute-start.4 = (f32[1,32896]{1,0:T(1,128)}, f32[1,32896]{1,0:T(1,128)}, u32[]{:S(2)}, u32[]{:S(2)}) collective-permute-start(f32[1,32896]{1,0:T(1,128)} %get-tuple-element.24), channel_id=1, source_target_pairs={{0,3},{1,4},{2,5},{3,6},{4,7},{5,0},{6,1},{7,2},{8,11},{9,12},{10,... | collective-permute-start | bytes 394760 | tf_op jit(solution)/shard_map/ppermute | solution.py:104
  69.6 13.3 %collective-permute-start.5 = (f32[1,32896]{1,0:T(1,128)}, f32[1,32896]{1,0:T(1,128)}, u32[]{:S(2)}, u32[]{:S(2)}) collective-permute-start(f32[1,32896]{1,0:T(1,128)} %get-tuple-element.23), channel_id=1, source_target_pairs={{0,4},{1,5},{2,6},{3,7},{4,0},{5,1},{6,2},{7,3},{8,12},{9,13},{10,... | collective-permute-start | bytes 394760 | tf_op jit(solution)/shard_map/ppermute | solution.py:104
  71.3 11.6 %collective-permute-start.6 = (f32[1,32896]{1,0:T(1,128)S(1)}, f32[1,32896]{1,0:T(1,128)}, u32[]{:S(2)}, u32[]{:S(2)}) collective-permute-start(f32[1,32896]{1,0:T(1,128)S(1)} %get-tuple-element.22), channel_id=1, source_target_pairs={{0,5},{1,6},{2,7},{3,0},{4,1},{5,2},{6,3},{7,4},{8,13},{9,14},{10,... | collective-permute-start | bytes 394760 | tf_op jit(solution)/shard_map/ppermute | solution.py:104
  78.1 0.6 copy-start.2
  78.1 5.4 %collective-permute-start.7 = (f32[1,32896]{1,0:T(1,128)S(1)}, f32[1,32896]{1,0:T(1,128)}, u32[]{:S(2)}, u32[]{:S(2)}) collective-permute-start(f32[1,32896]{1,0:T(1,128)S(1)} %get-tuple-element.21), channel_id=1, source_target_pairs={{0,6},{1,7},{2,0},{3,1},{4,2},{5,3},{6,4},{7,5},{8,14},{9,15},{10,... | collective-permute-start | bytes 394760 | tf_op jit(solution)/shard_map/ppermute | solution.py:104
  78.1 0.7 copy-start.3
  78.1 5.4 %collective-permute-start.8 = (f32[1,32896]{1,0:T(1,128)S(1)}, f32[1,32896]{1,0:T(1,128)}, u32[]{:S(2)}, u32[]{:S(2)}) collective-permute-start(f32[1,32896]{1,0:T(1,128)S(1)} %get-tuple-element.20), channel_id=1, source_target_pairs={{0,7},{1,0},{2,1},{3,2},{4,3},{5,4},{6,5},{7,6},{8,15},{9,8},{10,9... | collective-permute-start | bytes 394760 | tf_op jit(solution)/shard_map/ppermute | solution.py:104
  85.2 15.0 %copy-start.8 = (pred[8]{0:T(512)(128)(4,1)S(1)}, pred[8]{0:T(512)(128)(4,1)}, u32[]{:S(2)}) copy-start(pred[8]{0:T(512)(128)(4,1)} %compare_and_fusion) | copy-start | bytes 28
  87.2 7.2 %collective-permute-start.9 = (bf16[32,1152]{1,0:T(8,128)(2,1)S(1)}, bf16[32,1152]{1,0:T(8,128)(2,1)S(1)}, u32[]{:S(2)}, u32[]{:S(2)}) collective-permute-start(bf16[32,1152]{1,0:T(8,128)(2,1)S(1)} %concatenate.21), channel_id=1, source_target_pairs={{0,1},{1,2},{2,3},{3,4},{4,5},{5,6},{6,7},{7,0},{8,9},{9,10},{10,1... | collective-permute-start | bytes 221192 | tf_op jit(solution)/shard_map/ppermute | solution.py:128
  87.3 8.7 %collective-permute-start.10 = (bf16[32,1152]{1,0:T(8,128)(2,1)S(1)}, bf16[32,1152]{1,0:T(8,128)(2,1)S(1)}, u32[]{:S(2)}, u32[]{:S(2)}) collective-permute-start(bf16[32,1152]{1,0:T(8,128)(2,1)S(1)} %concatenate.21), channel_id=1, source_target_pairs={{0,2},{1,3},{2,4},{3,5},{4,6},{5,7},{6,0},{7,1},{8,10},{9,11},{10,... | collective-permute-start | bytes 221192 | tf_op jit(solution)/shard_map/ppermute | solution.py:128
  91.1 6.3 %collective-permute-start.11 = (bf16[32,1152]{1,0:T(8,128)(2,1)S(1)}, bf16[32,1152]{1,0:T(8,128)(2,1)S(1)}, u32[]{:S(2)}, u32[]{:S(2)}) collective-permute-start(bf16[32,1152]{1,0:T(8,128)(2,1)S(1)} %concatenate.21), channel_id=1, source_target_pairs={{0,3},{1,4},{2,5},{3,6},{4,7},{5,0},{6,1},{7,2},{8,11},{9,12},{10,... | collective-permute-start | bytes 221192 | tf_op jit(solution)/shard_map/ppermute | solution.py:128
  91.7 7.6 %collective-permute-start.12 = (bf16[32,1152]{1,0:T(8,128)(2,1)S(1)}, bf16[32,1152]{1,0:T(8,128)(2,1)S(1)}, u32[]{:S(2)}, u32[]{:S(2)}) collective-permute-start(bf16[32,1152]{1,0:T(8,128)(2,1)S(1)} %concatenate.21), channel_id=1, source_target_pairs={{0,4},{1,5},{2,6},{3,7},{4,0},{5,1},{6,2},{7,3},{8,12},{9,13},{10,... | collective-permute-start | bytes 221192 | tf_op jit(solution)/shard_map/ppermute | solution.py:128
  93.9 5.4 %collective-permute-start.13 = (bf16[32,1152]{1,0:T(8,128)(2,1)S(1)}, bf16[32,1152]{1,0:T(8,128)(2,1)S(1)}, u32[]{:S(2)}, u32[]{:S(2)}) collective-permute-start(bf16[32,1152]{1,0:T(8,128)(2,1)S(1)} %concatenate.21), channel_id=1, source_target_pairs={{0,5},{1,6},{2,7},{3,0},{4,1},{5,2},{6,3},{7,4},{8,13},{9,14},{10,... | collective-permute-start | bytes 221192 | tf_op jit(solution)/shard_map/ppermute | solution.py:128
  94.4 5.0 %collective-permute-start.14 = (bf16[32,1152]{1,0:T(8,128)(2,1)S(1)}, bf16[32,1152]{1,0:T(8,128)(2,1)S(1)}, u32[]{:S(2)}, u32[]{:S(2)}) collective-permute-start(bf16[32,1152]{1,0:T(8,128)(2,1)S(1)} %concatenate.21), channel_id=1, source_target_pairs={{0,6},{1,7},{2,0},{3,1},{4,2},{5,3},{6,4},{7,5},{8,14},{9,15},{10,... | collective-permute-start | bytes 221192 | tf_op jit(solution)/shard_map/ppermute | solution.py:128
  96.0 3.4 %collective-permute-start.15 = (bf16[32,1152]{1,0:T(8,128)(2,1)S(1)}, bf16[32,1152]{1,0:T(8,128)(2,1)S(1)}, u32[]{:S(2)}, u32[]{:S(2)}) collective-permute-start(bf16[32,1152]{1,0:T(8,128)(2,1)S(1)} %concatenate.21), channel_id=1, source_target_pairs={{0,7},{1,0},{2,1},{3,2},{4,3},{5,4},{6,5},{7,6},{8,15},{9,8},{10,9... | collective-permute-start | bytes 221192 | tf_op jit(solution)/shard_map/ppermute | solution.py:128
  100.3 5.9 %collective-permute-start.16 = (bf16[8,32,1152]{2,1,0:T(8,128)(2,1)S(1)}, bf16[8,32,1152]{2,1,0:T(8,128)(2,1)}, u32[]{:S(2)}, u32[]{:S(2)}) collective-permute-start(bf16[8,32,1152]{2,1,0:T(8,128)(2,1)S(1)} %broadcast_select_fusion.1), channel_id=1, source_target_pairs={{0,16},{16,0},{1,17},{17,1},{2,18},{18,2},{3,19},{19,3},{4,20},{20... | collective-permute-start | bytes 1769480 | tf_op jit(solution)/shard_map/ppermute | solution.py:133
  109.1 0.7 copy-start.5
  117.3 3.6 %collective-permute-start.17 = (f32[8,32896]{1,0:T(8,128)}, f32[8,32896]{1,0:T(8,128)}, u32[]{:S(2)}, u32[]{:S(2)}) collective-permute-start(f32[8,32896]{1,0:T(8,128)} %select_maximum_fusion), channel_id=1, source_target_pairs={{0,16},{16,0},{1,17},{17,1},{2,18},{18,2},{3,19},{19,3},{4,20},{20... | collective-permute-start | bytes 3158024 | tf_op jit(solution)/shard_map/ppermute | solution.py:99
  122.3 35.9 %copy-start.7 = (s32[512]{0:T(512)S(1)}, s32[512]{0:T(512)}, u32[]{:S(2)}) copy-start(s32[512]{0:T(512)} %copy-done.6) | copy-start | bytes 6148
  122.9 7.8 %collective-permute-start.18 = (f32[1,32896]{1,0:T(1,128)S(1)}, f32[1,32896]{1,0:T(1,128)S(1)}, u32[]{:S(2)}, u32[]{:S(2)}) collective-permute-start(f32[1,32896]{1,0:T(1,128)S(1)} %get-tuple-element.12), channel_id=1, source_target_pairs={{0,1},{1,2},{2,3},{3,4},{4,5},{5,6},{6,7},{7,0},{8,9},{9,10},{10,1... | collective-permute-start | bytes 394760 | tf_op jit(solution)/shard_map/ppermute | solution.py:104
  124.4 10.9 %collective-permute-start.19 = (f32[1,32896]{1,0:T(1,128)S(1)}, f32[1,32896]{1,0:T(1,128)S(1)}, u32[]{:S(2)}, u32[]{:S(2)}) collective-permute-start(f32[1,32896]{1,0:T(1,128)S(1)} %get-tuple-element.18), channel_id=1, source_target_pairs={{0,2},{1,3},{2,4},{3,5},{4,6},{5,7},{6,0},{7,1},{8,10},{9,11},{10,... | collective-permute-start | bytes 394760 | tf_op jit(solution)/shard_map/ppermute | solution.py:104
  128.4 25.5 %collective-permute-start.20 = (f32[1,32896]{1,0:T(1,128)S(1)}, f32[1,32896]{1,0:T(1,128)S(1)}, u32[]{:S(2)}, u32[]{:S(2)}) collective-permute-start(f32[1,32896]{1,0:T(1,128)S(1)} %get-tuple-element.17), channel_id=1, source_target_pairs={{0,3},{1,4},{2,5},{3,6},{4,7},{5,0},{6,1},{7,2},{8,11},{9,12},{10,... | collective-permute-start | bytes 394760 | tf_op jit(solution)/shard_map/ppermute | solution.py:104
  128.4 25.6 %collective-permute-start.21 = (f32[1,32896]{1,0:T(1,128)S(1)}, f32[1,32896]{1,0:T(1,128)S(1)}, u32[]{:S(2)}, u32[]{:S(2)}) collective-permute-start(f32[1,32896]{1,0:T(1,128)S(1)} %get-tuple-element.16), channel_id=1, source_target_pairs={{0,4},{1,5},{2,6},{3,7},{4,0},{5,1},{6,2},{7,3},{8,12},{9,13},{10,... | collective-permute-start | bytes 394760 | tf_op jit(solution)/shard_map/ppermute | solution.py:104
  128.5 25.5 %collective-permute-start.22 = (f32[1,32896]{1,0:T(1,128)S(1)}, f32[1,32896]{1,0:T(1,128)S(1)}, u32[]{:S(2)}, u32[]{:S(2)}) collective-permute-start(f32[1,32896]{1,0:T(1,128)S(1)} %get-tuple-element.15), channel_id=1, source_target_pairs={{0,5},{1,6},{2,7},{3,0},{4,1},{5,2},{6,3},{7,4},{8,13},{9,14},{10,... | collective-permute-start | bytes 394760 | tf_op jit(solution)/shard_map/ppermute | solution.py:104
  130.8 23.2 %collective-permute-start.23 = (f32[1,32896]{1,0:T(1,128)S(1)}, f32[1,32896]{1,0:T(1,128)S(1)}, u32[]{:S(2)}, u32[]{:S(2)}) collective-permute-start(f32[1,32896]{1,0:T(1,128)S(1)} %get-tuple-element.14), channel_id=1, source_target_pairs={{0,6},{1,7},{2,0},{3,1},{4,2},{5,3},{6,4},{7,5},{8,14},{9,15},{10,... | collective-permute-start | bytes 394760 | tf_op jit(solution)/shard_map/ppermute | solution.py:104
  135.4 18.6 %collective-permute-start.24 = (f32[1,32896]{1,0:T(1,128)S(1)}, f32[1,32896]{1,0:T(1,128)S(1)}, u32[]{:S(2)}, u32[]{:S(2)}) collective-permute-start(f32[1,32896]{1,0:T(1,128)S(1)} %get-tuple-element.13), channel_id=1, source_target_pairs={{0,7},{1,0},{2,1},{3,2},{4,3},{5,4},{6,5},{7,6},{8,15},{9,8},{10,9... | collective-permute-start | bytes 394760 | tf_op jit(solution)/shard_map/ppermute | solution.py:104
  154.9 7.8 %collective-permute-start.25 = (f32[32,1024]{1,0:T(8,128)S(1)}, f32[32,1024]{1,0:T(8,128)S(1)}, u32[]{:S(2)}, u32[]{:S(2)}) collective-permute-start(f32[32,1024]{1,0:T(8,128)S(1)} %add_divide_fusion), channel_id=1, source_target_pairs={{0,0},{8,16},{16,8},{24,24},{1,1},{9,17},{17,9},{25,25},{2,2},{10,... | collective-permute-start | bytes 393224 | tf_op jit(solution)/shard_map/ppermute | solution.py:146

commit v2 on v0

--- a/solution.py
+++ b/solution.py
@@ -118,14 +118,13 @@
                 ],
                 axis=1,
             )
-            by_shift = jnp.stack(
-                [block]
-                + [
-                    lax.ppermute(block, PLANE, [(i, (i + shift) % plane) for i in range(plane)])
-                    for shift in range(1, plane)
-                ]
+            on_plane = lax.all_to_all(
+                jnp.broadcast_to(block[None], (plane,) + block.shape),
+                PLANE,
+                split_axis=0,
+                concat_axis=0,
+                tiled=True,
             )
-            on_plane = jnp.take(by_shift, (spot - jnp.arange(plane)) % plane, axis=0)
             partner_plane = lax.ppermute(on_plane, "core", [(0, 1), (1, 0)])
             everyone = jnp.concatenate(
                 [

time: 152 us -> 151 us (level)
  blocking collectives: 16.4 us -> 30.8 us
  starting transfers between devices: 45.4 us -> 31 us
    all_to_all x0 -> x1, blocking collectives: none -> 11.8 us  [steps(): lax.all_to_all(jnp.broadcast_to(block[None], (plane,) + block.shape), PLA...]
    ppermute x7 -> x0, starting transfers between devices: 9.28 us -> none  [steps(): lax.ppermute(block, PLANE, [(i, (i + shift) % plane) for i in range(plane)])]
    ppermute x14, starting transfers between devices: 13.3 us -> 9.34 us  [steps(): lax.ppermute(outgoing, PLANE, [(i, (i + shift) % plane) for i in range(pl...]
    ppermute x14, waiting for transfers between devices: 14.9 us -> 17.8 us  [steps(): lax.ppermute(outgoing, PLANE, [(i, (i + shift) % plane) for i in range(pl...]
    ppermute x7 -> x0, waiting for transfers between devices: 2.58 us -> none  [steps(): lax.ppermute(block, PLANE, [(i, (i + shift) % plane) for i in range(plane)])]
    all_to_all x1, blocking collectives: 16.4 us -> 18.9 us  [steps(): lax.all_to_all(smoothing_scale * closing_log_partition, ROUTE, split_axis...]
  transfers between devices with their start and end apart: 27 -> 20, of which waited for: 14 -> 11; matrix products, arithmetic and copies ran while one was open for 4% -> 4% of each run, Pallas kernels for 0% -> 0%
where the time goes in v2:
time: 151 us
  waiting for transfers between devices  53.9 us (36%)
  starting transfers between devices  31 us (21%)
  blocking collectives  30.8 us (20%)
  other arithmetic  14.3 us (9%)
  matrix products  10.5 us (7%)
  local copies, waits for them, and re-layouts  9.51 us (6%)
    all_to_all x1, waiting for transfers between devices, steps(): lax.all_to_all(packed, ROUTE, split_axis=0, concat_axis=0, tiled=True)  23.7 us
    all_to_all x1, blocking collectives, steps(): lax.all_to_all(smoothing_scale * closing_log_partition, ROUTE, split_axis...  18.9 us
    ppermute x14, waiting for transfers between devices, steps(): lax.ppermute(outgoing, PLANE, [(i, (i + shift) % plane) for i in range(pl...  17.8 us
    all_to_all x1, blocking collectives, steps(): lax.all_to_all(jnp.broadcast_to(block[None], (plane,) + block.shape), PLA...  11.8 us
    all_to_all x1, starting transfers between devices, steps(): lax.all_to_all(packed, ROUTE, split_axis=0, concat_axis=0, tiled=True)  11.5 us
    ppermute x14, starting transfers between devices, steps(): lax.ppermute(outgoing, PLANE, [(i, (i + shift) % plane) for i in range(pl...  9.34 us
    dot_general x2, matrix products, steps(): jnp.einsum('rk,rd->kd', weights, arrived, preferred_element_type=jnp.floa...  5.22 us
    ppermute x2, waiting for transfers between devices, steps(): halves = mine + lax.ppermute(theirs, 'core', [(0, 1), (1, 0)])  4.72 us
  transfers between devices with their start and end apart: 20, of which 11 were waited for; matrix products, arithmetic and copies ran while one was open for 4% of the time, Pallas kernels for 0%

profile of v2, /device:TPU:1, one launch (start us, length us, event | category | flops | bytes accessed | tf_op | source)
XLA Modules:
  0.0 150.9 jit_solution(13795630999702439776)
XLA Ops:
  0.7 0.9 copy.27
  1.8 0.9 fusion.27
  2.8 0.7 multiply_add_fusion
  4.1 2.7 %select_bitcast_fusion = bf16[128,8,1024]{2,1,0:T(8,128)(2,1)} fusion(pred[1024]{0:T(1024)(128)(4,1)S(1)} %broadcast_compare_fusion, bf16[512,1024]{1,0:T(8,128)(2,1)S(1)} %copy-done.2, bf16[1024]{0:T(1024)(128)(2,1)S(1)} %fusion.31, f32[512]{0:T(512)S(1)} %add_rsqrt_fusion, s32[512]{0:T(512)S(1)} %multiply_add_fusion), kind=kOutput, calls=%fused_computation.19 | convolution fusion | flops 1078460416 | bytes 3152896 | tf_op jit(solution)/shard_map/dot_general | solution.py:58
  6.8 11.5 %all-to-all-start = ((bf16[128,8,1024]{2,1,0:T(8,128)(2,1)}), bf16[128,8,1024]{2,1,0:T(8,128)(2,1)S(1)}, u32[]{:S(2)}, u32[]{:S(2)}) async-start(bf16[128,8,1024]{2,1,0:T(8,128)(2,1)} %select_bitcast_fusion), calls=%async_computation | async-start | bytes 4194304 | tf_op jit(solution)/shard_map/all_to_all | solution.py:62
  18.3 1.1 collective-permute-start
  19.4 2.4 %collective-permute-done = bf16[512,1024]{1,0:T(8,128)(2,1)} collective-permute-done((bf16[512,1024]{1,0:T(8,128)(2,1)S(1)}, bf16[512,1024]{1,0:T(8,128)(2,1)}, u32[]{:S(2)}, u32[]{:S(2)}) %collective-permute-start) | collective-permute-done | bytes 1048608 | tf_op jit(solution)/shard_map/ppermute | solution.py:37
  21.9 2.8 %fusion.43 = (f32[512,1024]{1,0:T(8,128)}, bf16[512,1024]{1,0:T(8,128)(2,1)S(1)}) fusion(bf16[512,1024]{1,0:T(8,128)(2,1)} %param.5, bf16[512,1024]{1,0:T(8,128)(2,1)} %collective-permute-done, pred[]{:T(512)S(6)} %eq.88), kind=kLoop, calls=%fused_computation.114 | loop fusion | flops 1048576 | bytes 5242881 | tf_op jit(solution)/shard_map/convert_element_type | solution.py:64
  24.9 23.7 %all-to-all-done = bf16[128,8,1024]{2,1,0:T(8,128)(2,1)S(1)} async-done(((bf16[128,8,1024]{2,1,0:T(8,128)(2,1)}), bf16[128,8,1024]{2,1,0:T(8,128)(2,1)S(1)}, u32[]{:S(2)}, u32[]{:S(2)}) %all-to-all-start) | async-done | bytes 2097184 | tf_op jit(solution)/shard_map/all_to_all | solution.py:62
  48.7 1.3 fusion.5
  50.0 0.5 fusion.7
  50.5 0.8 convert_reduce_fusion.1
  51.3 2.6 %fusion.38 = f32[512,1024]{1,0:T(8,128)} fusion(bf16[1024,512]{0,1:T(8,128)(2,1)S(1)} %get-tuple-element.9, bf16[128,8,1024]{2,1,0:T(8,128)(2,1)S(1)} %all-to-all-done), kind=kOutput, calls=%fused_computation.109 | convolution fusion | flops 1073741824 | bytes 5242880 | tf_op jit(solution)/shard_map/rk,rd->kd/dot_general | solution.py:83
  53.9 1.7 %concatenate.23 = f32[2,8,32768]{2,1,0:T(8,128)S(1)} reshape(f32[512,1024]{1,0:T(8,128)} %fusion.38) | data formatting | bytes 4194304 | tf_op jit(solution)/shard_map/concatenate | solution.py:85
  55.9 1.3 collective-permute-start.1
  57.2 2.4 %collective-permute-done.1 = f32[8,32896]{1,0:T(8,128)} collective-permute-done((f32[8,32896]{1,0:T(8,128)S(1)}, f32[8,32896]{1,0:T(8,128)}, u32[]{:S(2)}, u32[]{:S(2)}) %collective-permute-start.1) | collective-permute-done | bytes 1052704 | tf_op jit(solution)/shard_map/ppermute | solution.py:96
  59.6 1.3 fusion.18
  61.0 0.6 constant_dynamic-slice_fusion.12
  62.0 1.3 collective-permute-start.3
  63.3 0.6 collective-permute-start.4
  63.9 1.7 %collective-permute-start.5 = (f32[1,32896]{1,0:T(1,128)S(1)}, f32[1,32896]{1,0:T(1,128)S(1)}, u32[]{:S(2)}, u32[]{:S(2)}) collective-permute-start(f32[1,32896]{1,0:T(1,128)S(1)} %get-tuple-element.23), channel_id=1, source_target_pairs={{0,4},{1,5},{2,6},{3,7},{4,0},{5,1},{6,2},{7,3},{8,12},{9,13},{10,... | collective-permute-start | bytes 394760 | tf_op jit(solution)/shard_map/ppermute | solution.py:100
  66.0 6.8 %collective-permute-done.2 = f32[1,32896]{1,0:T(1,128)S(1)} collective-permute-done((f32[1,32896]{1,0:T(1,128)S(1)}, f32[1,32896]{1,0:T(1,128)S(1)}, u32[]{:S(2)}, u32[]{:S(2)}) %collective-permute-start.2) | collective-permute-done | bytes 131616 | tf_op jit(solution)/shard_map/ppermute | solution.py:100
  73.2 4.5 %collective-permute-done.5 = f32[1,32896]{1,0:T(1,128)S(1)} collective-permute-done((f32[1,32896]{1,0:T(1,128)S(1)}, f32[1,32896]{1,0:T(1,128)S(1)}, u32[]{:S(2)}, u32[]{:S(2)}) %collective-permute-start.5) | collective-permute-done | bytes 131616 | tf_op jit(solution)/shard_map/ppermute | solution.py:100
  79.0 1.1 multiply_reduce_fusion.1
  80.6 11.8 %all_to_all.23 = bf16[8,32,1152]{2,1,0:T(8,128)(2,1)S(1)} all-to-all(bf16[8,32,1152]{2,1,0:T(8,128)(2,1)S(1)} %broadcast_in_dim.43), channel_id=1, replica_groups=mesh['z'=4,'core'=2,'yhi'=2,'ylo'=2,'x'=4] {'ylo','x'}, dimensions={0} | all-to-all | bytes 1179648 | tf_op jit(solution)/shard_map/all_to_all | solution.py:121
  92.4 4.0 %collective-permute-start.9 = (bf16[8,32,1152]{2,1,0:T(8,128)(2,1)S(1)}, bf16[8,32,1152]{2,1,0:T(8,128)(2,1)S(1)}, u32[]{:S(2)}, u32[]{:S(2)}) collective-permute-start(bf16[8,32,1152]{2,1,0:T(8,128)(2,1)S(1)} %all_to_all.23), channel_id=1, source_target_pairs={{0,16},{16,0},{1,17},{17,1},{2,18},{18,2},{3,19},{19,3},{4,20},{20... | collective-permute-start | bytes 1769480 | tf_op jit(solution)/shard_map/ppermute | solution.py:128
  96.4 1.6 %collective-permute-done.9 = bf16[8,32,1152]{2,1,0:T(8,128)(2,1)S(1)} collective-permute-done((bf16[8,32,1152]{2,1,0:T(8,128)(2,1)S(1)}, bf16[8,32,1152]{2,1,0:T(8,128)(2,1)S(1)}, u32[]{:S(2)}, u32[]{:S(2)}) %collective-permute-start.9) | collective-permute-done | bytes 589856 | tf_op jit(solution)/shard_map/ppermute | solution.py:128
  98.6 1.1 copy-done.1
  99.7 1.3 fusion.6
  101.1 0.5 fusion.8
  101.5 0.8 convert_reduce_fusion
  102.4 2.6 %fusion.35 = f32[512,1024]{1,0:T(8,128)} fusion(bf16[1024,512]{0,1:T(8,128)(2,1)S(1)} %get-tuple-element.3, bf16[128,8,1024]{2,1,0:T(8,128)(2,1)S(1)} %copy-done.1), kind=kOutput, calls=%fused_computation.106 | convolution fusion | flops 1073741824 | bytes 5242880 | tf_op jit(solution)/shard_map/rk,rd->kd/dot_general | solution.py:83
  105.0 1.7 %concatenate.28 = f32[2,8,32768]{2,1,0:T(8,128)S(1)} reshape(f32[512,1024]{1,0:T(8,128)} %fusion.35) | data formatting | bytes 4194304 | tf_op jit(solution)/shard_map/concatenate | solution.py:85
  107.3 2.3 %collective-permute-done.10 = f32[8,32896]{1,0:T(8,128)S(1)} collective-permute-done((f32[8,32896]{1,0:T(8,128)S(1)}, f32[8,32896]{1,0:T(8,128)S(1)}, u32[]{:S(2)}, u32[]{:S(2)}) %collective-permute-start.10) | collective-permute-done | bytes 1052704 | tf_op jit(solution)/shard_map/ppermute | solution.py:96
  109.7 0.6 constant_dynamic-slice_fusion.5
  110.4 0.5 collective-permute-start.11
  110.9 1.7 %collective-permute-start.12 = (f32[1,32896]{1,0:T(1,128)S(1)}, f32[1,32896]{1,0:T(1,128)S(1)}, u32[]{:S(2)}, u32[]{:S(2)}) collective-permute-start(f32[1,32896]{1,0:T(1,128)S(1)} %get-tuple-element.18), channel_id=1, source_target_pairs={{0,2},{1,3},{2,4},{3,5},{4,6},{5,7},{6,0},{7,1},{8,10},{9,11},{10,... | collective-permute-start | bytes 394760 | tf_op jit(solution)/shard_map/ppermute | solution.py:100
  112.6 0.8 collective-permute-start.13
  113.4 1.2 collective-permute-start.14
  114.6 0.7 collective-permute-start.15
  115.4 5.7 %collective-permute-done.11 = f32[1,32896]{1,0:T(1,128)S(1)} collective-permute-done((f32[1,32896]{1,0:T(1,128)S(1)}, f32[1,32896]{1,0:T(1,128)S(1)}, u32[]{:S(2)}, u32[]{:S(2)}) %collective-permute-start.11) | collective-permute-done | bytes 131616 | tf_op jit(solution)/shard_map/ppermute | solution.py:100
  121.1 18.9 %all_to_all.24 = f32[128,8,1]{1,2,0:T(1,128)S(1)} all-to-all(f32[128,8,1]{1,2,0:T(1,128)S(1)} %bitcast.68), channel_id=1, replica_groups=mesh['z'=4,'core'=2,'yhi'=2,'ylo'=2,'x'=4] {'z','yhi','core','ylo','x'}, dimensions={0} | all-to-all | bytes 8192 | tf_op jit(solution)/shard_map/all_to_all | solution.py:79
  140.1 0.5 broadcast.143
  140.6 0.8 reduce.15
  142.5 3.2 %collective-permute-start.18 = (f32[32,1024]{1,0:T(8,128)S(1)}, f32[32,1024]{1,0:T(8,128)S(1)}, u32[]{:S(2)}, u32[]{:S(2)}) collective-permute-start(f32[32,1024]{1,0:T(8,128)S(1)} %add_divide_fusion), channel_id=1, source_target_pairs={{0,0},{8,16},{16,8},{24,24},{1,1},{9,17},{17,9},{25,25},{2,2},{10,... | collective-permute-start | bytes 393224 | tf_op jit(solution)/shard_map/ppermute | solution.py:141
  145.7 0.9 select_reduce_fusion
  146.6 3.7 %collective-permute-done.18 = f32[32,1024]{1,0:T(8,128)S(1)} collective-permute-done((f32[32,1024]{1,0:T(8,128)S(1)}, f32[32,1024]{1,0:T(8,128)S(1)}, u32[]{:S(2)}, u32[]{:S(2)}) %collective-permute-start.18) | collective-permute-done | bytes 131104 | tf_op jit(solution)/shard_map/ppermute | solution.py:141
  150.3 0.7 copy.34
  (71 shorter events, 6.7 us)
Async XLA Ops:
  0.6 3.1 %copy-start.2 = (bf16[512,1024]{1,0:T(8,128)(2,1)S(1)}, bf16[512,1024]{1,0:T(8,128)(2,1)}, u32[]{:S(2)}) copy-start(bf16[512,1024]{1,0:T(8,128)(2,1)} %param.3) | copy-start | bytes 3145732
  6.8 11.5 %copy-start.3 = (bf16[512,1024]{1,0:T(8,128)(2,1)S(1)}, bf16[512,1024]{1,0:T(8,128)(2,1)}, u32[]{:S(2)}) copy-start(bf16[512,1024]{1,0:T(8,128)(2,1)} %param.5) | copy-start | bytes 3145732
  6.8 41.8 %all-to-all-start = ((bf16[128,8,1024]{2,1,0:T(8,128)(2,1)}), bf16[128,8,1024]{2,1,0:T(8,128)(2,1)S(1)}, u32[]{:S(2)}, u32[]{:S(2)}) async-start(bf16[128,8,1024]{2,1,0:T(8,128)(2,1)} %select_bitcast_fusion), calls=%async_computation | async-start | bytes 4194304 | tf_op jit(solution)/shard_map/all_to_all | solution.py:62
  18.3 3.6 %collective-permute-start = (bf16[512,1024]{1,0:T(8,128)(2,1)S(1)}, bf16[512,1024]{1,0:T(8,128)(2,1)}, u32[]{:S(2)}, u32[]{:S(2)}) collective-permute-start(bf16[512,1024]{1,0:T(8,128)(2,1)S(1)} %copy-done.3), channel_id=1, source_target_pairs={{0,16},{16,0},{1,17},{17,1},{2,18},{18,2},{3,19},{19,3},{4,20},{20... | collective-permute-start | bytes 3145736 | tf_op jit(solution)/shard_map/ppermute | solution.py:37
  48.6 2.8 %copy-start = (bf16[128,8,1024]{2,1,0:T(8,128)(2,1)}, bf16[128,8,1024]{2,1,0:T(8,128)(2,1)S(1)}, u32[]{:S(2)}) copy-start(bf16[128,8,1024]{2,1,0:T(8,128)(2,1)S(1)} %all-to-all-done) | copy-start | bytes 6291460
  55.9 3.8 %collective-permute-start.1 = (f32[8,32896]{1,0:T(8,128)S(1)}, f32[8,32896]{1,0:T(8,128)}, u32[]{:S(2)}, u32[]{:S(2)}) collective-permute-start(f32[8,32896]{1,0:T(8,128)S(1)} %fusion.15), channel_id=1, source_target_pairs={{0,16},{16,0},{1,17},{17,1},{2,18},{18,2},{3,19},{19,3},{4,20},{20... | collective-permute-start | bytes 3158024 | tf_op jit(solution)/shard_map/ppermute | solution.py:96
  61.6 11.2 %collective-permute-start.2 = (f32[1,32896]{1,0:T(1,128)S(1)}, f32[1,32896]{1,0:T(1,128)S(1)}, u32[]{:S(2)}, u32[]{:S(2)}) collective-permute-start(f32[1,32896]{1,0:T(1,128)S(1)} %get-tuple-element.19), channel_id=1, source_target_pairs={{0,1},{1,2},{2,3},{3,4},{4,5},{5,6},{6,7},{7,0},{8,9},{9,10},{10,1... | collective-permute-start | bytes 394760 | tf_op jit(solution)/shard_map/ppermute | solution.py:100
  62.0 10.8 %collective-permute-start.3 = (f32[1,32896]{1,0:T(1,128)S(1)}, f32[1,32896]{1,0:T(1,128)S(1)}, u32[]{:S(2)}, u32[]{:S(2)}) collective-permute-start(f32[1,32896]{1,0:T(1,128)S(1)} %get-tuple-element.25), channel_id=1, source_target_pairs={{0,2},{1,3},{2,4},{3,5},{4,6},{5,7},{6,0},{7,1},{8,10},{9,11},{10,... | collective-permute-start | bytes 394760 | tf_op jit(solution)/shard_map/ppermute | solution.py:100
  63.3 9.9 %collective-permute-start.4 = (f32[1,32896]{1,0:T(1,128)S(1)}, f32[1,32896]{1,0:T(1,128)S(1)}, u32[]{:S(2)}, u32[]{:S(2)}) collective-permute-start(f32[1,32896]{1,0:T(1,128)S(1)} %get-tuple-element.24), channel_id=1, source_target_pairs={{0,3},{1,4},{2,5},{3,6},{4,7},{5,0},{6,1},{7,2},{8,11},{9,12},{10,... | collective-permute-start | bytes 394760 | tf_op jit(solution)/shard_map/ppermute | solution.py:100
  63.9 13.8 %collective-permute-start.5 = (f32[1,32896]{1,0:T(1,128)S(1)}, f32[1,32896]{1,0:T(1,128)S(1)}, u32[]{:S(2)}, u32[]{:S(2)}) collective-permute-start(f32[1,32896]{1,0:T(1,128)S(1)} %get-tuple-element.23), channel_id=1, source_target_pairs={{0,4},{1,5},{2,6},{3,7},{4,0},{5,1},{6,2},{7,3},{8,12},{9,13},{10,... | collective-permute-start | bytes 394760 | tf_op jit(solution)/shard_map/ppermute | solution.py:100
  65.7 12.0 %collective-permute-start.6 = (f32[1,32896]{1,0:T(1,128)S(1)}, f32[1,32896]{1,0:T(1,128)S(1)}, u32[]{:S(2)}, u32[]{:S(2)}) collective-permute-start(f32[1,32896]{1,0:T(1,128)S(1)} %get-tuple-element.22), channel_id=1, source_target_pairs={{0,5},{1,6},{2,7},{3,0},{4,1},{5,2},{6,3},{7,4},{8,13},{9,14},{10,... | collective-permute-start | bytes 394760 | tf_op jit(solution)/shard_map/ppermute | solution.py:100
  72.8 5.3 %collective-permute-start.7 = (f32[1,32896]{1,0:T(1,128)S(1)}, f32[1,32896]{1,0:T(1,128)S(1)}, u32[]{:S(2)}, u32[]{:S(2)}) collective-permute-start(f32[1,32896]{1,0:T(1,128)S(1)} %get-tuple-element.21), channel_id=1, source_target_pairs={{0,6},{1,7},{2,0},{3,1},{4,2},{5,3},{6,4},{7,5},{8,14},{9,15},{10,... | collective-permute-start | bytes 394760 | tf_op jit(solution)/shard_map/ppermute | solution.py:100
  72.8 5.3 %collective-permute-start.8 = (f32[1,32896]{1,0:T(1,128)S(1)}, f32[1,32896]{1,0:T(1,128)S(1)}, u32[]{:S(2)}, u32[]{:S(2)}) collective-permute-start(f32[1,32896]{1,0:T(1,128)S(1)} %get-tuple-element.20), channel_id=1, source_target_pairs={{0,7},{1,0},{2,1},{3,2},{4,3},{5,4},{6,5},{7,6},{8,15},{9,8},{10,9... | collective-permute-start | bytes 394760 | tf_op jit(solution)/shard_map/ppermute | solution.py:100
  92.4 5.6 %collective-permute-start.9 = (bf16[8,32,1152]{2,1,0:T(8,128)(2,1)S(1)}, bf16[8,32,1152]{2,1,0:T(8,128)(2,1)S(1)}, u32[]{:S(2)}, u32[]{:S(2)}) collective-permute-start(bf16[8,32,1152]{2,1,0:T(8,128)(2,1)S(1)} %all_to_all.23), channel_id=1, source_target_pairs={{0,16},{16,0},{1,17},{17,1},{2,18},{18,2},{3,19},{19,3},{4,20},{20... | collective-permute-start | bytes 1769480 | tf_op jit(solution)/shard_map/ppermute | solution.py:128
  98.2 1.6 %copy-start.1 = (bf16[128,8,1024]{2,1,0:T(8,128)(2,1)S(1)}, bf16[128,8,1024]{2,1,0:T(8,128)(2,1)}, u32[]{:S(2)}) copy-start(bf16[128,8,1024]{2,1,0:T(8,128)(2,1)} %copy-done) | copy-start | bytes 6291460
  106.9 2.7 %collective-permute-start.10 = (f32[8,32896]{1,0:T(8,128)S(1)}, f32[8,32896]{1,0:T(8,128)S(1)}, u32[]{:S(2)}, u32[]{:S(2)}) collective-permute-start(f32[8,32896]{1,0:T(8,128)S(1)} %fusion.10), channel_id=1, source_target_pairs={{0,16},{16,0},{1,17},{17,1},{2,18},{18,2},{3,19},{19,3},{4,20},{20... | collective-permute-start | bytes 3158024 | tf_op jit(solution)/shard_map/ppermute | solution.py:96
  110.4 10.6 %collective-permute-start.11 = (f32[1,32896]{1,0:T(1,128)S(1)}, f32[1,32896]{1,0:T(1,128)S(1)}, u32[]{:S(2)}, u32[]{:S(2)}) collective-permute-start(f32[1,32896]{1,0:T(1,128)S(1)} %get-tuple-element.12), channel_id=1, source_target_pairs={{0,1},{1,2},{2,3},{3,4},{4,5},{5,6},{6,7},{7,0},{8,9},{9,10},{10,1... | collective-permute-start | bytes 394760 | tf_op jit(solution)/shard_map/ppermute | solution.py:100
  110.9 10.1 %collective-permute-start.12 = (f32[1,32896]{1,0:T(1,128)S(1)}, f32[1,32896]{1,0:T(1,128)S(1)}, u32[]{:S(2)}, u32[]{:S(2)}) collective-permute-start(f32[1,32896]{1,0:T(1,128)S(1)} %get-tuple-element.18), channel_id=1, source_target_pairs={{0,2},{1,3},{2,4},{3,5},{4,6},{5,7},{6,0},{7,1},{8,10},{9,11},{10,... | collective-permute-start | bytes 394760 | tf_op jit(solution)/shard_map/ppermute | solution.py:100
  112.6 28.9 %collective-permute-start.13 = (f32[1,32896]{1,0:T(1,128)S(1)}, f32[1,32896]{1,0:T(1,128)S(1)}, u32[]{:S(2)}, u32[]{:S(2)}) collective-permute-start(f32[1,32896]{1,0:T(1,128)S(1)} %get-tuple-element.17), channel_id=1, source_target_pairs={{0,3},{1,4},{2,5},{3,6},{4,7},{5,0},{6,1},{7,2},{8,11},{9,12},{10,... | collective-permute-start | bytes 394760 | tf_op jit(solution)/shard_map/ppermute | solution.py:100
  113.4 28.1 %collective-permute-start.14 = (f32[1,32896]{1,0:T(1,128)S(1)}, f32[1,32896]{1,0:T(1,128)S(1)}, u32[]{:S(2)}, u32[]{:S(2)}) collective-permute-start(f32[1,32896]{1,0:T(1,128)S(1)} %get-tuple-element.16), channel_id=1, source_target_pairs={{0,4},{1,5},{2,6},{3,7},{4,0},{5,1},{6,2},{7,3},{8,12},{9,13},{10,... | collective-permute-start | bytes 394760 | tf_op jit(solution)/shard_map/ppermute | solution.py:100
  114.6 26.9 %collective-permute-start.15 = (f32[1,32896]{1,0:T(1,128)S(1)}, f32[1,32896]{1,0:T(1,128)S(1)}, u32[]{:S(2)}, u32[]{:S(2)}) collective-permute-start(f32[1,32896]{1,0:T(1,128)S(1)} %get-tuple-element.15), channel_id=1, source_target_pairs={{0,5},{1,6},{2,7},{3,0},{4,1},{5,2},{6,3},{7,4},{8,13},{9,14},{10,... | collective-permute-start | bytes 394760 | tf_op jit(solution)/shard_map/ppermute | solution.py:100
  121.0 20.5 %collective-permute-start.16 = (f32[1,32896]{1,0:T(1,128)S(1)}, f32[1,32896]{1,0:T(1,128)S(1)}, u32[]{:S(2)}, u32[]{:S(2)}) collective-permute-start(f32[1,32896]{1,0:T(1,128)S(1)} %get-tuple-element.14), channel_id=1, source_target_pairs={{0,6},{1,7},{2,0},{3,1},{4,2},{5,3},{6,4},{7,5},{8,14},{9,15},{10,... | collective-permute-start | bytes 394760 | tf_op jit(solution)/shard_map/ppermute | solution.py:100
  121.0 20.5 %collective-permute-start.17 = (f32[1,32896]{1,0:T(1,128)S(1)}, f32[1,32896]{1,0:T(1,128)S(1)}, u32[]{:S(2)}, u32[]{:S(2)}) collective-permute-start(f32[1,32896]{1,0:T(1,128)S(1)} %get-tuple-element.13), channel_id=1, source_target_pairs={{0,7},{1,0},{2,1},{3,2},{4,3},{5,4},{6,5},{7,6},{8,15},{9,8},{10,9... | collective-permute-start | bytes 394760 | tf_op jit(solution)/shard_map/ppermute | solution.py:100
  142.5 7.8 %collective-permute-start.18 = (f32[32,1024]{1,0:T(8,128)S(1)}, f32[32,1024]{1,0:T(8,128)S(1)}, u32[]{:S(2)}, u32[]{:S(2)}) collective-permute-start(f32[32,1024]{1,0:T(8,128)S(1)} %add_divide_fusion), channel_id=1, source_target_pairs={{0,0},{8,16},{16,8},{24,24},{1,1},{9,17},{17,9},{25,25},{2,2},{10,... | collective-permute-start | bytes 393224 | tf_op jit(solution)/shard_map/ppermute | solution.py:141

commit v3 on v2

--- a/solution.py
+++ b/solution.py
@@ -32,7 +32,6 @@
     share_rows = K // members
     core = lax.axis_index("core")
     yhi = lax.axis_index("yhi")
-    spot = lax.axis_index(PLANE)
     first_row = lax.axis_index(TEAM) * share_rows
     partner = lax.ppermute(centroid_seeds, "core", [(0, 1), (1, 0)])
     seeds16 = jnp.where(core == yhi, centroid_seeds, partner)
@@ -94,12 +93,18 @@
         mine = lax.dynamic_index_in_dim(by_core, core, 0, keepdims=False)
         theirs = lax.dynamic_index_in_dim(by_core, 1 - core, 0, keepdims=False)
         halves = mine + lax.ppermute(theirs, "core", [(0, 1), (1, 0)])
-        reduced = lax.dynamic_index_in_dim(halves, spot, 0, keepdims=True)
-        for shift in range(1, plane):
-            outgoing = lax.dynamic_index_in_dim(halves, (spot + shift) % plane, 0, keepdims=True)
-            incoming = lax.ppermute(
-                outgoing, PLANE, [(i, (i + shift) % plane) for i in range(plane)]
-            )
+        lanes = lax.axis_size("x")
+        ylo = lax.axis_index("ylo")
+        column = lax.axis_index("x")
+        by_row = halves.reshape(-1, lanes, halves.shape[1])
+        mine_row = lax.dynamic_index_in_dim(by_row, ylo, 0, keepdims=False)
+        other_row = lax.dynamic_index_in_dim(by_row, 1 - ylo, 0, keepdims=False)
+        other_row = lax.ppermute(other_row, "ylo", [(0, 1), (1, 0)])
+        row_sums = mine_row + other_row
+        reduced = lax.dynamic_index_in_dim(row_sums, column, 0, keepdims=True)
+        for shift in range(1, lanes):
+            outgoing = lax.dynamic_index_in_dim(row_sums, (column + shift) % lanes, 0, keepdims=True)
+            incoming = lax.ppermute(outgoing, "x", [(i, (i + shift) % lanes) for i in range(lanes)])
             reduced = reduced + incoming
         weighted_own = reduced[0, : share_rows * features].reshape(share_rows, features)
         masses_own = reduced[0, share_rows * features : share_rows * features + share_rows]

time: 151 us -> 162 us (1.073)
  waiting for transfers between devices: 53.9 us -> 67.5 us
  starting transfers between devices: 31 us -> 26.1 us
    ppermute x14 -> x8, waiting for transfers between devices: 17.8 us -> 31.4 us  [the longest x2 26 us: steps(): other_row = lax.ppermute(other_row, 'ylo', [(0, 1), (1, 0)])]
    ppermute x14 -> x8, starting transfers between devices: 9.34 us -> 6.28 us  [the longest x6 5.83 us: steps(): lax.ppermute(outgoing, 'x', [(i, (i + shift) % lanes) for i in range(lane...]
    all_to_all x1, blocking collectives: 11.8 us -> 14.6 us  [steps(): lax.all_to_all(jnp.broadcast_to(block[None], (plane,) + block.shape), PLA...]
    ppermute x1, starting transfers between devices: 3.99 us -> 2.18 us  [steps(): partner_plane = lax.ppermute(on_plane, 'core', [(0, 1), (1, 0)])]
  transfers between devices with their start and end apart: 20 -> 14, of which waited for: 11 -> 11; matrix products, arithmetic and copies ran while one was open for 4% -> 3% of each run, Pallas kernels for 0% -> 0%
where the time goes in v3:
time: 162 us; the launch traced here: 161 us
  waiting for transfers between devices  67.5 us (42%)
  blocking collectives  32.3 us (20%)
  starting transfers between devices  26.1 us (16%)
  other arithmetic  14.2 us (9%)
  matrix products  10.5 us (6%)
  local copies, waits for them, and re-layouts  9.63 us (6%)
    ppermute x2, waiting for transfers between devices, steps(): other_row = lax.ppermute(other_row, 'ylo', [(0, 1), (1, 0)])  26 us
    all_to_all x1, waiting for transfers between devices, steps(): lax.all_to_all(packed, ROUTE, split_axis=0, concat_axis=0, tiled=True)  23.7 us
    all_to_all x1, blocking collectives, steps(): lax.all_to_all(smoothing_scale * closing_log_partition, ROUTE, split_axis...  17.7 us
    all_to_all x1, blocking collectives, steps(): lax.all_to_all(jnp.broadcast_to(block[None], (plane,) + block.shape), PLA...  14.6 us
    all_to_all x1, starting transfers between devices, steps(): lax.all_to_all(packed, ROUTE, split_axis=0, concat_axis=0, tiled=True)  11.5 us
    ppermute x6, starting transfers between devices, steps(): lax.ppermute(outgoing, 'x', [(i, (i + shift) % lanes) for i in range(lane...  5.83 us
    ppermute x6, waiting for transfers between devices, steps(): lax.ppermute(outgoing, 'x', [(i, (i + shift) % lanes) for i in range(lane...  5.48 us
    dot_general x2, matrix products, steps(): jnp.einsum('rk,rd->kd', weights, arrived, preferred_element_type=jnp.floa...  5.22 us
  transfers between devices with their start and end apart: 14, of which 11 were waited for; matrix products, arithmetic and copies ran while one was open for 3% of the time, Pallas kernels for 0%

profile of v3, /device:TPU:1, one launch (start us, length us, event | category | flops | bytes accessed | tf_op | source)
XLA Modules:
  0.0 161.3 jit_solution(2996422328044893003)
XLA Ops:
  0.7 0.9 copy.27
  1.8 0.9 fusion.27
  2.8 0.7 multiply_add_fusion
  4.1 2.7 %select_bitcast_fusion = bf16[128,8,1024]{2,1,0:T(8,128)(2,1)} fusion(pred[1024]{0:T(1024)(128)(4,1)S(1)} %broadcast_compare_fusion, bf16[512,1024]{1,0:T(8,128)(2,1)S(1)} %copy-done.2, bf16[1024]{0:T(1024)(128)(2,1)S(1)} %fusion.31, f32[512]{0:T(512)S(1)} %add_rsqrt_fusion, s32[512]{0:T(512)S(1)} %multiply_add_fusion), kind=kOutput, calls=%fused_computation.19 | convolution fusion | flops 1078460416 | bytes 3152896 | tf_op jit(solution)/shard_map/dot_general | solution.py:57
  6.8 11.5 %all-to-all-start = ((bf16[128,8,1024]{2,1,0:T(8,128)(2,1)}), bf16[128,8,1024]{2,1,0:T(8,128)(2,1)S(1)}, u32[]{:S(2)}, u32[]{:S(2)}) async-start(bf16[128,8,1024]{2,1,0:T(8,128)(2,1)} %select_bitcast_fusion), calls=%async_computation | async-start | bytes 4194304 | tf_op jit(solution)/shard_map/all_to_all | solution.py:61
  18.3 1.1 collective-permute-start
  19.4 2.4 %collective-permute-done = bf16[512,1024]{1,0:T(8,128)(2,1)} collective-permute-done((bf16[512,1024]{1,0:T(8,128)(2,1)S(1)}, bf16[512,1024]{1,0:T(8,128)(2,1)}, u32[]{:S(2)}, u32[]{:S(2)}) %collective-permute-start) | collective-permute-done | bytes 1048608 | tf_op jit(solution)/shard_map/ppermute | solution.py:36
  21.9 2.8 %fusion.43 = (f32[512,1024]{1,0:T(8,128)}, bf16[512,1024]{1,0:T(8,128)(2,1)S(1)}) fusion(bf16[512,1024]{1,0:T(8,128)(2,1)} %param.5, bf16[512,1024]{1,0:T(8,128)(2,1)} %collective-permute-done, pred[]{:T(512)S(6)} %eq.80), kind=kLoop, calls=%fused_computation.110 | loop fusion | flops 1048576 | bytes 5242881 | tf_op jit(solution)/shard_map/convert_element_type | solution.py:63
  24.9 23.7 %all-to-all-done = bf16[128,8,1024]{2,1,0:T(8,128)(2,1)S(1)} async-done(((bf16[128,8,1024]{2,1,0:T(8,128)(2,1)}), bf16[128,8,1024]{2,1,0:T(8,128)(2,1)S(1)}, u32[]{:S(2)}, u32[]{:S(2)}) %all-to-all-start) | async-done | bytes 2097184 | tf_op jit(solution)/shard_map/all_to_all | solution.py:61
  48.7 1.3 fusion.5
  50.0 0.5 fusion.7
  50.5 0.8 convert_reduce_fusion.1
  51.3 2.6 %fusion.38 = f32[512,1024]{1,0:T(8,128)} fusion(bf16[1024,512]{0,1:T(8,128)(2,1)S(1)} %get-tuple-element.9, bf16[128,8,1024]{2,1,0:T(8,128)(2,1)S(1)} %all-to-all-done), kind=kOutput, calls=%fused_computation.105 | convolution fusion | flops 1073741824 | bytes 5242880 | tf_op jit(solution)/shard_map/rk,rd->kd/dot_general | solution.py:82
  53.9 1.7 %concatenate.23 = f32[2,8,32768]{2,1,0:T(8,128)S(1)} reshape(f32[512,1024]{1,0:T(8,128)} %fusion.38) | data formatting | bytes 4194304 | tf_op jit(solution)/shard_map/concatenate | solution.py:84
  55.9 1.3 collective-permute-start.1
  57.2 2.4 %collective-permute-done.1 = f32[8,32896]{1,0:T(8,128)} collective-permute-done((f32[8,32896]{1,0:T(8,128)S(1)}, f32[8,32896]{1,0:T(8,128)}, u32[]{:S(2)}, u32[]{:S(2)}) %collective-permute-start.1) | collective-permute-done | bytes 1052704 | tf_op jit(solution)/shard_map/ppermute | solution.py:95
  59.6 1.3 fusion.18
  61.5 13.1 %collective-permute-done.2 = f32[4,32896]{1,0:T(4,128)S(1)} collective-permute-done((f32[4,32896]{1,0:T(4,128)S(1)}, f32[4,32896]{1,0:T(4,128)S(1)}, u32[]{:S(2)}, u32[]{:S(2)}) %collective-permute-start.2) | collective-permute-done | bytes 526368 | tf_op jit(solution)/shard_map/ppermute | solution.py:102
  74.7 0.3 constant_dynamic-slice_fusion.4
  75.1 0.4 collective-permute-start.3
  75.4 1.3 collective-permute-start.4
  76.7 1.2 collective-permute-start.5
  77.9 3.9 %collective-permute-done.3 = f32[1,32896]{1,0:T(1,128)S(1)} collective-permute-done((f32[1,32896]{1,0:T(1,128)S(1)}, f32[1,32896]{1,0:T(1,128)S(1)}, u32[]{:S(2)}, u32[]{:S(2)}) %collective-permute-start.3) | collective-permute-done | bytes 131616 | tf_op jit(solution)/shard_map/ppermute | solution.py:107
  81.8 0.3 collective-permute-done.4
  82.2 1.2 collective-permute-done.5
  84.1 1.1 multiply_reduce_fusion.1
  85.7 14.6 %all_to_all.23 = bf16[8,32,1152]{2,1,0:T(8,128)(2,1)S(1)} all-to-all(bf16[8,32,1152]{2,1,0:T(8,128)(2,1)S(1)} %broadcast_in_dim.43), channel_id=1, replica_groups=mesh['z'=4,'core'=2,'yhi'=2,'ylo'=2,'x'=4] {'ylo','x'}, dimensions={0} | all-to-all | bytes 1179648 | tf_op jit(solution)/shard_map/all_to_all | solution.py:126
  100.2 2.2 %collective-permute-start.6 = (bf16[8,32,1152]{2,1,0:T(8,128)(2,1)S(1)}, bf16[8,32,1152]{2,1,0:T(8,128)(2,1)S(1)}, u32[]{:S(2)}, u32[]{:S(2)}) collective-permute-start(bf16[8,32,1152]{2,1,0:T(8,128)(2,1)S(1)} %all_to_all.23), channel_id=1, source_target_pairs={{0,16},{16,0},{1,17},{17,1},{2,18},{18,2},{3,19},{19,3},{4,20},{20... | collective-permute-start | bytes 1769480 | tf_op jit(solution)/shard_map/ppermute | solution.py:133
  102.4 1.6 %collective-permute-done.6 = bf16[8,32,1152]{2,1,0:T(8,128)(2,1)S(1)} collective-permute-done((bf16[8,32,1152]{2,1,0:T(8,128)(2,1)S(1)}, bf16[8,32,1152]{2,1,0:T(8,128)(2,1)S(1)}, u32[]{:S(2)}, u32[]{:S(2)}) %collective-permute-start.6) | collective-permute-done | bytes 589856 | tf_op jit(solution)/shard_map/ppermute | solution.py:133
  104.6 1.1 copy-done.1
  105.7 1.3 fusion.6
  107.1 0.5 fusion.8
  107.5 0.8 convert_reduce_fusion
  108.3 2.6 %fusion.35 = f32[512,1024]{1,0:T(8,128)} fusion(bf16[1024,512]{0,1:T(8,128)(2,1)S(1)} %get-tuple-element.3, bf16[128,8,1024]{2,1,0:T(8,128)(2,1)S(1)} %copy-done.1), kind=kOutput, calls=%fused_computation.102 | convolution fusion | flops 1073741824 | bytes 5242880 | tf_op jit(solution)/shard_map/rk,rd->kd/dot_general | solution.py:82
  111.0 1.7 %concatenate.28 = f32[2,8,32768]{2,1,0:T(8,128)S(1)} reshape(f32[512,1024]{1,0:T(8,128)} %fusion.35) | data formatting | bytes 4194304 | tf_op jit(solution)/shard_map/concatenate | solution.py:84
  112.9 0.5 collective-permute-start.7
  113.3 2.3 %collective-permute-done.7 = f32[8,32896]{1,0:T(8,128)S(1)} collective-permute-done((f32[8,32896]{1,0:T(8,128)S(1)}, f32[8,32896]{1,0:T(8,128)S(1)}, u32[]{:S(2)}, u32[]{:S(2)}) %collective-permute-start.7) | collective-permute-done | bytes 1052704 | tf_op jit(solution)/shard_map/ppermute | solution.py:95
  116.1 0.4 collective-permute-start.8
  116.5 12.9 %collective-permute-done.8 = f32[4,32896]{1,0:T(4,128)S(1)} collective-permute-done((f32[4,32896]{1,0:T(4,128)S(1)}, f32[4,32896]{1,0:T(4,128)S(1)}, u32[]{:S(2)}, u32[]{:S(2)}) %collective-permute-start.8) | collective-permute-done | bytes 526368 | tf_op jit(solution)/shard_map/ppermute | solution.py:102
  129.8 1.0 collective-permute-start.10
  130.9 2.0 %collective-permute-start.11 = (f32[1,32896]{1,0:T(1,128)S(1)}, f32[1,32896]{1,0:T(1,128)S(1)}, u32[]{:S(2)}, u32[]{:S(2)}) collective-permute-start(f32[1,32896]{1,0:T(1,128)S(1)} %get-tuple-element.13), channel_id=1, source_target_pairs={{0,3},{1,0},{2,1},{3,2},{4,7},{5,4},{6,5},{7,6},{8,11},{9,8},{10,9... | collective-permute-start | bytes 394760 | tf_op jit(solution)/shard_map/ppermute | solution.py:107
  132.9 17.7 %all_to_all.24 = f32[128,8,1]{1,2,0:T(1,128)S(1)} all-to-all(f32[128,8,1]{1,2,0:T(1,128)S(1)} %bitcast.76), channel_id=1, replica_groups=mesh['z'=4,'core'=2,'yhi'=2,'ylo'=2,'x'=4] {'z','yhi','core','ylo','x'}, dimensions={0} | all-to-all | bytes 8192 | tf_op jit(solution)/shard_map/all_to_all | solution.py:78
  150.6 0.5 broadcast.139
  151.1 0.8 reduce.15
  152.9 3.2 %collective-permute-start.12 = (f32[32,1024]{1,0:T(8,128)S(1)}, f32[32,1024]{1,0:T(8,128)S(1)}, u32[]{:S(2)}, u32[]{:S(2)}) collective-permute-start(f32[32,1024]{1,0:T(8,128)S(1)} %add_divide_fusion), channel_id=1, source_target_pairs={{0,0},{8,16},{16,8},{24,24},{1,1},{9,17},{17,9},{25,25},{2,2},{10,... | collective-permute-start | bytes 393224 | tf_op jit(solution)/shard_map/ppermute | solution.py:146
  156.1 0.9 select_reduce_fusion
  157.0 3.7 %collective-permute-done.12 = f32[32,1024]{1,0:T(8,128)S(1)} collective-permute-done((f32[32,1024]{1,0:T(8,128)S(1)}, f32[32,1024]{1,0:T(8,128)S(1)}, u32[]{:S(2)}, u32[]{:S(2)}) %collective-permute-start.12) | collective-permute-done | bytes 131104 | tf_op jit(solution)/shard_map/ppermute | solution.py:146
  160.7 0.7 copy.34
  (65 shorter events, 5.8 us)
Async XLA Ops:
  0.6 3.1 %copy-start.2 = (bf16[512,1024]{1,0:T(8,128)(2,1)S(1)}, bf16[512,1024]{1,0:T(8,128)(2,1)}, u32[]{:S(2)}) copy-start(bf16[512,1024]{1,0:T(8,128)(2,1)} %param.3) | copy-start | bytes 3145732
  6.8 11.5 %copy-start.3 = (bf16[512,1024]{1,0:T(8,128)(2,1)S(1)}, bf16[512,1024]{1,0:T(8,128)(2,1)}, u32[]{:S(2)}) copy-start(bf16[512,1024]{1,0:T(8,128)(2,1)} %param.5) | copy-start | bytes 3145732
  6.8 41.8 %all-to-all-start = ((bf16[128,8,1024]{2,1,0:T(8,128)(2,1)}), bf16[128,8,1024]{2,1,0:T(8,128)(2,1)S(1)}, u32[]{:S(2)}, u32[]{:S(2)}) async-start(bf16[128,8,1024]{2,1,0:T(8,128)(2,1)} %select_bitcast_fusion), calls=%async_computation | async-start | bytes 4194304 | tf_op jit(solution)/shard_map/all_to_all | solution.py:61
  18.3 3.6 %collective-permute-start = (bf16[512,1024]{1,0:T(8,128)(2,1)S(1)}, bf16[512,1024]{1,0:T(8,128)(2,1)}, u32[]{:S(2)}, u32[]{:S(2)}) collective-permute-start(bf16[512,1024]{1,0:T(8,128)(2,1)S(1)} %copy-done.3), channel_id=1, source_target_pairs={{0,16},{16,0},{1,17},{17,1},{2,18},{18,2},{3,19},{19,3},{4,20},{20... | collective-permute-start | bytes 3145736 | tf_op jit(solution)/shard_map/ppermute | solution.py:36
  48.6 2.8 %copy-start = (bf16[128,8,1024]{2,1,0:T(8,128)(2,1)}, bf16[128,8,1024]{2,1,0:T(8,128)(2,1)S(1)}, u32[]{:S(2)}) copy-start(bf16[128,8,1024]{2,1,0:T(8,128)(2,1)S(1)} %all-to-all-done) | copy-start | bytes 6291460
  55.9 3.8 %collective-permute-start.1 = (f32[8,32896]{1,0:T(8,128)S(1)}, f32[8,32896]{1,0:T(8,128)}, u32[]{:S(2)}, u32[]{:S(2)}) collective-permute-start(f32[8,32896]{1,0:T(8,128)S(1)} %fusion.15), channel_id=1, source_target_pairs={{0,16},{16,0},{1,17},{17,1},{2,18},{18,2},{3,19},{19,3},{4,20},{20... | collective-permute-start | bytes 3158024 | tf_op jit(solution)/shard_map/ppermute | solution.py:95
  61.3 13.2 %collective-permute-start.2 = (f32[4,32896]{1,0:T(4,128)S(1)}, f32[4,32896]{1,0:T(4,128)S(1)}, u32[]{:S(2)}, u32[]{:S(2)}) collective-permute-start(f32[4,32896]{1,0:T(4,128)S(1)} %dynamic-slice_bitcast_fusion.1), channel_id=1, source_target_pairs={{0,4},{4,0},{1,5},{5,1},{2,6},{6,2},{3,7},{7,3},{8,12},{12,8},{9,1... | collective-permute-start | bytes 1579016 | tf_op jit(solution)/shard_map/ppermute | solution.py:102
  75.1 6.8 %collective-permute-start.3 = (f32[1,32896]{1,0:T(1,128)S(1)}, f32[1,32896]{1,0:T(1,128)S(1)}, u32[]{:S(2)}, u32[]{:S(2)}) collective-permute-start(f32[1,32896]{1,0:T(1,128)S(1)} %get-tuple-element.15), channel_id=1, source_target_pairs={{0,1},{1,2},{2,3},{3,0},{4,5},{5,6},{6,7},{7,4},{8,9},{9,10},{10,1... | collective-permute-start | bytes 394760 | tf_op jit(solution)/shard_map/ppermute | solution.py:107
  75.4 6.7 %collective-permute-start.4 = (f32[1,32896]{1,0:T(1,128)S(1)}, f32[1,32896]{1,0:T(1,128)S(1)}, u32[]{:S(2)}, u32[]{:S(2)}) collective-permute-start(f32[1,32896]{1,0:T(1,128)S(1)} %get-tuple-element.17), channel_id=1, source_target_pairs={{0,2},{1,3},{2,0},{3,1},{4,6},{5,7},{6,4},{7,5},{8,10},{9,11},{10,... | collective-permute-start | bytes 394760 | tf_op jit(solution)/shard_map/ppermute | solution.py:107
  76.7 6.7 %collective-permute-start.5 = (f32[1,32896]{1,0:T(1,128)S(1)}, f32[1,32896]{1,0:T(1,128)S(1)}, u32[]{:S(2)}, u32[]{:S(2)}) collective-permute-start(f32[1,32896]{1,0:T(1,128)S(1)} %get-tuple-element.16), channel_id=1, source_target_pairs={{0,3},{1,0},{2,1},{3,2},{4,7},{5,4},{6,5},{7,6},{8,11},{9,8},{10,9... | collective-permute-start | bytes 394760 | tf_op jit(solution)/shard_map/ppermute | solution.py:107
  100.2 3.8 %collective-permute-start.6 = (bf16[8,32,1152]{2,1,0:T(8,128)(2,1)S(1)}, bf16[8,32,1152]{2,1,0:T(8,128)(2,1)S(1)}, u32[]{:S(2)}, u32[]{:S(2)}) collective-permute-start(bf16[8,32,1152]{2,1,0:T(8,128)(2,1)S(1)} %all_to_all.23), channel_id=1, source_target_pairs={{0,16},{16,0},{1,17},{17,1},{2,18},{18,2},{3,19},{19,3},{4,20},{20... | collective-permute-start | bytes 1769480 | tf_op jit(solution)/shard_map/ppermute | solution.py:133
  104.2 1.6 copy-start.1
  112.9 2.7 %collective-permute-start.7 = (f32[8,32896]{1,0:T(8,128)S(1)}, f32[8,32896]{1,0:T(8,128)S(1)}, u32[]{:S(2)}, u32[]{:S(2)}) collective-permute-start(f32[8,32896]{1,0:T(8,128)S(1)} %fusion.10), channel_id=1, source_target_pairs={{0,16},{16,0},{1,17},{17,1},{2,18},{18,2},{3,19},{19,3},{4,20},{20... | collective-permute-start | bytes 3158024 | tf_op jit(solution)/shard_map/ppermute | solution.py:95
  116.1 13.2 %collective-permute-start.8 = (f32[4,32896]{1,0:T(4,128)S(1)}, f32[4,32896]{1,0:T(4,128)S(1)}, u32[]{:S(2)}, u32[]{:S(2)}) collective-permute-start(f32[4,32896]{1,0:T(4,128)S(1)} %dynamic-slice_bitcast_fusion), channel_id=1, source_target_pairs={{0,4},{4,0},{1,5},{5,1},{2,6},{6,2},{3,7},{7,3},{8,12},{12,8},{9,1... | collective-permute-start | bytes 1579016 | tf_op jit(solution)/shard_map/ppermute | solution.py:102
  129.8 22.2 %collective-permute-start.10 = (f32[1,32896]{1,0:T(1,128)S(1)}, f32[1,32896]{1,0:T(1,128)S(1)}, u32[]{:S(2)}, u32[]{:S(2)}) collective-permute-start(f32[1,32896]{1,0:T(1,128)S(1)} %get-tuple-element.14), channel_id=1, source_target_pairs={{0,2},{1,3},{2,0},{3,1},{4,6},{5,7},{6,4},{7,5},{8,10},{9,11},{10,... | collective-permute-start | bytes 394760 | tf_op jit(solution)/shard_map/ppermute | solution.py:107
  130.9 21.2 %collective-permute-start.11 = (f32[1,32896]{1,0:T(1,128)S(1)}, f32[1,32896]{1,0:T(1,128)S(1)}, u32[]{:S(2)}, u32[]{:S(2)}) collective-permute-start(f32[1,32896]{1,0:T(1,128)S(1)} %get-tuple-element.13), channel_id=1, source_target_pairs={{0,3},{1,0},{2,1},{3,2},{4,7},{5,4},{6,5},{7,6},{8,11},{9,8},{10,9... | collective-permute-start | bytes 394760 | tf_op jit(solution)/shard_map/ppermute | solution.py:107
  132.8 19.3 %collective-permute-start.9 = (f32[1,32896]{1,0:T(1,128)S(1)}, f32[1,32896]{1,0:T(1,128)S(1)}, u32[]{:S(2)}, u32[]{:S(2)}) collective-permute-start(f32[1,32896]{1,0:T(1,128)S(1)} %get-tuple-element.12), channel_id=1, source_target_pairs={{0,1},{1,2},{2,3},{3,0},{4,5},{5,6},{6,7},{7,4},{8,9},{9,10},{10,1... | collective-permute-start | bytes 394760 | tf_op jit(solution)/shard_map/ppermute | solution.py:107
  152.9 7.8 %collective-permute-start.12 = (f32[32,1024]{1,0:T(8,128)S(1)}, f32[32,1024]{1,0:T(8,128)S(1)}, u32[]{:S(2)}, u32[]{:S(2)}) collective-permute-start(f32[32,1024]{1,0:T(8,128)S(1)} %add_divide_fusion), channel_id=1, source_target_pairs={{0,0},{8,16},{16,8},{24,24},{1,1},{9,17},{17,9},{25,25},{2,2},{10,... | collective-permute-start | bytes 393224 | tf_op jit(solution)/shard_map/ppermute | solution.py:146

commit v4 on v2

--- a/solution.py
+++ b/solution.py
@@ -61,6 +61,14 @@
     packed = jnp.where(filled[:, None], gathered, empty_row[None, :])
     arrived = lax.all_to_all(packed, ROUTE, split_axis=0, concat_axis=0, tiled=True)
     slot_mask = (arrived[:, 0].astype(jnp.float32) < 1.5).astype(jnp.float32)
+    widened_rows = jnp.concatenate(
+        [
+            arrived,
+            jnp.ones((arrived.shape[0], 1), jnp.bfloat16),
+            jnp.zeros((arrived.shape[0], 127), jnp.bfloat16),
+        ],
+        axis=1,
+    )
     seeds = seeds16.astype(jnp.float32)
     own = lax.dynamic_slice_in_dim(seeds, first_row, share_rows, 0)
     prototype_lowbits = seeds16
@@ -80,17 +88,10 @@
                 smoothing_scale * closing_log_partition, ROUTE, split_axis=0, concat_axis=0,
                 tiled=True,
             )
-        weighted = jnp.einsum("rk,rd->kd", weights, arrived, preferred_element_type=jnp.float32)
-        masses = jnp.sum(weights.astype(jnp.float32), axis=0)
-        combined = jnp.concatenate(
-            [
-                weighted.reshape(members, share_rows * features),
-                jnp.pad(masses.reshape(members, share_rows), ((0, 0), (0, 128 - share_rows))),
-            ],
-            axis=1,
+        weighted = jnp.einsum(
+            "rk,rd->kd", weights, widened_rows, preferred_element_type=jnp.float32
         )
-        width = combined.shape[1]
-        by_core = combined.reshape(cores, plane, width)
+        by_core = weighted.reshape(cores, plane, share_rows, features + 128)
         mine = lax.dynamic_index_in_dim(by_core, core, 0, keepdims=False)
         theirs = lax.dynamic_index_in_dim(by_core, 1 - core, 0, keepdims=False)
         halves = mine + lax.ppermute(theirs, "core", [(0, 1), (1, 0)])
@@ -101,8 +102,8 @@
                 outgoing, PLANE, [(i, (i + shift) % plane) for i in range(plane)]
             )
             reduced = reduced + incoming
-        weighted_own = reduced[0, : share_rows * features].reshape(share_rows, features)
-        masses_own = reduced[0, share_rows * features : share_rows * features + share_rows]
+        weighted_own = reduced[0, :, :features]
+        masses_own = reduced[0, :, features]
         own = (weighted_own + prior_mass * own) / (masses_own + prior_mass)[:, None]
         if iteration + 1 < ITERS:
             half_own = 0.5 * jnp.sum(own * own, axis=1)

time: 151 us -> 155 us (1.026)
  waiting for transfers between devices: 53.9 us -> 56.8 us
    ppermute x14, waiting for transfers between devices: 17.8 us -> 20.4 us  [steps(): lax.ppermute(outgoing, PLANE, [(i, (i + shift) % plane) for i in range(pl...]
    reduce_sum x2 -> x0, other arithmetic: 1.61 us -> none  [steps(): masses = jnp.sum(weights.astype(jnp.float32), axis=0)]
    unnamed x10 -> x12, local copies, waits for them, and re-layouts: 1.8 us -> 3.36 us
    concatenate x4 -> x1, local copies, waits for them, and re-layouts: 3.51 us -> 3.06 us  [steps(): jnp.concatenate([arrived, jnp.ones((arrived.shape[0], 1), jnp.bfloat16),...]
  transfers between devices with their start and end apart: 20 -> 20, of which waited for: 11 -> 12; matrix products, arithmetic and copies ran while one was open for 4% -> 4% of each run, Pallas kernels for 0% -> 0%
where the time goes in v4:
time: 155 us; the launch traced here: 154 us
  waiting for transfers between devices  56.8 us (37%)
  blocking collectives  31 us (20%)
  starting transfers between devices  30.7 us (20%)
  other arithmetic  13.6 us (9%)
  matrix products  11.3 us (7%)
  local copies, waits for them, and re-layouts  9.71 us (6%)
    all_to_all x1, waiting for transfers between devices, steps(): lax.all_to_all(packed, ROUTE, split_axis=0, concat_axis=0, tiled=True)  23.6 us
    ppermute x14, waiting for transfers between devices, steps(): lax.ppermute(outgoing, PLANE, [(i, (i + shift) % plane) for i in range(pl...  20.4 us
    all_to_all x1, blocking collectives, steps(): lax.all_to_all(smoothing_scale * closing_log_partition, ROUTE, split_axis...  19.1 us
    all_to_all x1, blocking collectives, steps(): lax.all_to_all(jnp.broadcast_to(block[None], (plane,) + block.shape), PLA...  11.9 us
    all_to_all x1, starting transfers between devices, steps(): lax.all_to_all(packed, ROUTE, split_axis=0, concat_axis=0, tiled=True)  11.5 us
    ppermute x14, starting transfers between devices, steps(): lax.ppermute(outgoing, PLANE, [(i, (i + shift) % plane) for i in range(pl...  9.28 us
    dot_general x2, matrix products, steps(): jnp.einsum('rk,rd->kd', weights, widened_rows, preferred_element_type=jnp...  5.94 us
    ppermute x2, waiting for transfers between devices, steps(): halves = mine + lax.ppermute(theirs, 'core', [(0, 1), (1, 0)])  5.08 us
  transfers between devices with their start and end apart: 20, of which 12 were waited for; matrix products, arithmetic and copies ran while one was open for 4% of the time, Pallas kernels for 0%

profile of v4, /device:TPU:1, one launch (start us, length us, event | category | flops | bytes accessed | tf_op | source)
XLA Modules:
  0.0 154.2 jit_solution(2691991118873602552)
XLA Ops:
  0.7 0.9 copy.27
  1.8 0.9 fusion.29
  2.8 0.7 multiply_add_fusion
  4.1 2.8 %select_bitcast_fusion = bf16[128,8,1024]{2,1,0:T(8,128)(2,1)} fusion(pred[1024]{0:T(1024)(128)(4,1)S(1)} %broadcast_compare_fusion, bf16[512,1024]{1,0:T(8,128)(2,1)S(1)} %copy-done.3, bf16[1024]{0:T(1024)(128)(2,1)S(1)} %fusion.39, f32[512]{0:T(512)S(1)} %add_rsqrt_fusion, s32[512]{0:T(512)S(1)} %multiply_add_fusion), kind=kOutput, calls=%fused_computation.13 | convolution fusion | flops 1078460416 | bytes 3152896 | tf_op jit(solution)/shard_map/dot_general | solution.py:58
  6.8 11.5 %all-to-all-start = ((bf16[128,8,1024]{2,1,0:T(8,128)(2,1)}), bf16[128,8,1024]{2,1,0:T(8,128)(2,1)S(1)}, u32[]{:S(2)}, u32[]{:S(2)}) async-start(bf16[128,8,1024]{2,1,0:T(8,128)(2,1)} %select_bitcast_fusion), calls=%async_computation | async-start | bytes 4194304 | tf_op jit(solution)/shard_map/all_to_all | solution.py:62
  18.3 1.1 collective-permute-start
  19.5 2.4 %collective-permute-done = bf16[512,1024]{1,0:T(8,128)(2,1)} collective-permute-done((bf16[512,1024]{1,0:T(8,128)(2,1)S(1)}, bf16[512,1024]{1,0:T(8,128)(2,1)}, u32[]{:S(2)}, u32[]{:S(2)}) %collective-permute-start) | collective-permute-done | bytes 1048608 | tf_op jit(solution)/shard_map/ppermute | solution.py:37
  21.9 2.8 %fusion.48 = (f32[512,1024]{1,0:T(8,128)}, bf16[512,1024]{1,0:T(8,128)(2,1)S(1)}) fusion(bf16[512,1024]{1,0:T(8,128)(2,1)} %param.5, bf16[512,1024]{1,0:T(8,128)(2,1)} %collective-permute-done, pred[]{:T(512)S(6)} %eq.88), kind=kLoop, calls=%fused_computation.108 | loop fusion | flops 1048576 | bytes 5242881 | tf_op jit(solution)/shard_map/convert_element_type | solution.py:72
  25.0 23.6 %all-to-all-done = bf16[128,8,1024]{2,1,0:T(8,128)(2,1)S(1)} async-done(((bf16[128,8,1024]{2,1,0:T(8,128)(2,1)}), bf16[128,8,1024]{2,1,0:T(8,128)(2,1)S(1)}, u32[]{:S(2)}, u32[]{:S(2)}) %all-to-all-start) | async-done | bytes 2097184 | tf_op jit(solution)/shard_map/all_to_all | solution.py:62
  48.8 1.3 fusion.5
  50.1 1.3 copy-done.2
  51.4 0.5 fusion.7
  52.0 3.1 %concatenate.10 = bf16[1024,1152]{1,0:T(8,128)(2,1)} concatenate(bf16[1024,1024]{1,0:T(8,128)(2,1)S(1)} %bitcast.63, bf16[1024,1]{1,0:T(8,128)(2,1)S(1)} %broadcast_in_dim.76, bf16[1024,127]{1,0:T(8,128)(2,1)S(1)} %broadcast_in_dim.77), dimensions={1} | concatenate | bytes 4718592 | tf_op jit(solution)/shard_map/concatenate | solution.py:64
  55.1 4.1 %fusion.9 = f32[512,1152]{1,0:T(8,128)S(1)} fusion(bf16[1024,1152]{1,0:T(8,128)(2,1)} %concatenate.10, f32[1024,512]{0,1:T(8,128)} %copy-done.2, f32[1024]{0:T(1024)S(1)} %convert_reduce_fusion.1, f32[1024]{0:T(1024)S(1)} %fusion.7, f32[1024]{0:T(1024)S(1)} %get-tuple-element.25, f32[512]{0:T(512)S(1)} %broadcast_multiply_fusion), kind=kOutput, calls=%fused_computation.27 | convolution fusion | flops 1211105280 | bytes 6830080 | tf_op jit(solution)/shard_map/rk,rd->kd/dot_general | solution.py:91
  59.2 1.4 copy-done.1
  60.6 1.3 collective-permute-start.1
  62.0 2.6 %collective-permute-done.1 = f32[8,32,1152]{2,1,0:T(8,128)} collective-permute-done((f32[8,32,1152]{2,1,0:T(8,128)S(1)}, f32[8,32,1152]{2,1,0:T(8,128)}, u32[]{:S(2)}, u32[]{:S(2)}) %collective-permute-start.1) | collective-permute-done | bytes 1179680 | tf_op jit(solution)/shard_map/ppermute | solution.py:97
  64.6 1.7 %bitcast_add_fusion.1 = f32[8,32,1152]{2,1,0:T(8,128)S(1)} fusion(f32[8,32,1152]{2,1,0:T(8,128)} %collective-permute-done.1, f32[2,8,32,1152]{3,2,1,0:T(8,128)} %bitcast.65, s32[]{:T(128)S(6)} %select_n.131), kind=kLoop, calls=%fused_computation.24 | loop fusion | flops 294912 | bytes 3538948 | tf_op jit(solution)/shard_map/add | solution.py:97
  66.3 0.9 constant_dynamic-slice_fusion.12
  67.6 1.3 collective-permute-start.3
  68.9 0.6 collective-permute-start.4
  69.5 1.7 %collective-permute-start.5 = (f32[1,32,1152]{2,1,0:T(8,128)}, f32[1,32,1152]{2,1,0:T(8,128)}, u32[]{:S(2)}, u32[]{:S(2)}) collective-permute-start(f32[1,32,1152]{2,1,0:T(8,128)} %get-tuple-element.19), channel_id=1, source_target_pairs={{0,4},{1,5},{2,6},{3,7},{4,0},{5,1},{6,2},{7,3},{8,12},{9,13},{10,... | collective-permute-start | bytes 442376 | tf_op jit(solution)/shard_map/ppermute | solution.py:101
  71.6 7.6 %collective-permute-done.2 = f32[1,32,1152]{2,1,0:T(8,128)S(1)} collective-permute-done((f32[1,32,1152]{2,1,0:T(8,128)S(1)}, f32[1,32,1152]{2,1,0:T(8,128)S(1)}, u32[]{:S(2)}, u32[]{:S(2)}) %collective-permute-start.2) | collective-permute-done | bytes 147488 | tf_op jit(solution)/shard_map/ppermute | solution.py:101
  79.2 0.9 collective-permute-done.4
  80.1 4.6 %collective-permute-done.5 = f32[1,32,1152]{2,1,0:T(8,128)} collective-permute-done((f32[1,32,1152]{2,1,0:T(8,128)}, f32[1,32,1152]{2,1,0:T(8,128)}, u32[]{:S(2)}, u32[]{:S(2)}) %collective-permute-start.5) | collective-permute-done | bytes 147488 | tf_op jit(solution)/shard_map/ppermute | solution.py:101
  85.3 1.3 add_add_fusion.1
  86.7 1.1 multiply_reduce_fusion.1
  88.4 11.9 %all_to_all.23 = bf16[8,32,1152]{2,1,0:T(8,128)(2,1)S(1)} all-to-all(bf16[8,32,1152]{2,1,0:T(8,128)(2,1)S(1)} %broadcast_in_dim.79), channel_id=1, replica_groups=mesh['z'=4,'core'=2,'yhi'=2,'ylo'=2,'x'=4] {'ylo','x'}, dimensions={0} | all-to-all | bytes 1179648 | tf_op jit(solution)/shard_map/all_to_all | solution.py:122
  100.3 3.7 %collective-permute-start.9 = (bf16[8,32,1152]{2,1,0:T(8,128)(2,1)S(1)}, bf16[8,32,1152]{2,1,0:T(8,128)(2,1)S(1)}, u32[]{:S(2)}, u32[]{:S(2)}) collective-permute-start(bf16[8,32,1152]{2,1,0:T(8,128)(2,1)S(1)} %all_to_all.23), channel_id=1, source_target_pairs={{0,16},{16,0},{1,17},{17,1},{2,18},{18,2},{3,19},{19,3},{4,20},{20... | collective-permute-start | bytes 1769480 | tf_op jit(solution)/shard_map/ppermute | solution.py:129
  104.0 1.6 %collective-permute-done.9 = bf16[8,32,1152]{2,1,0:T(8,128)(2,1)S(1)} collective-permute-done((bf16[8,32,1152]{2,1,0:T(8,128)(2,1)S(1)}, bf16[8,32,1152]{2,1,0:T(8,128)(2,1)S(1)}, u32[]{:S(2)}, u32[]{:S(2)}) %collective-permute-start.9) | collective-permute-done | bytes 589856 | tf_op jit(solution)/shard_map/ppermute | solution.py:129
  106.3 1.3 fusion.6
  107.6 0.5 fusion.8
  108.1 1.8 %fusion.10 = f32[512,1152]{1,0:T(8,128)S(1)} fusion(bf16[1024,1152]{1,0:T(8,128)(2,1)S(1)} %copy-done, f32[1024,512]{0,1:T(8,128)S(1)} %get-tuple-element.28, f32[1024]{0:T(1024)S(1)} %fusion.8, f32[1024]{0:T(1024)S(1)} %get-tuple-element.27, f32[512]{0:T(512)S(1)} %fusion.27, f32[1024]{0:T(1024)S(1)} %convert_reduce_fusion.1), kind=kOutput, calls=%fused_computation.28 | convolution fusion | flops 1211105280 | bytes 6830080 | tf_op jit(solution)/shard_map/rk,rd->kd/dot_general | solution.py:91
  110.0 0.5 collective-permute-start.10
  110.5 2.5 %collective-permute-done.10 = f32[8,32,1152]{2,1,0:T(8,128)S(1)} collective-permute-done((f32[8,32,1152]{2,1,0:T(8,128)S(1)}, f32[8,32,1152]{2,1,0:T(8,128)S(1)}, u32[]{:S(2)}, u32[]{:S(2)}) %collective-permute-start.10) | collective-permute-done | bytes 1179680 | tf_op jit(solution)/shard_map/ppermute | solution.py:97
  113.2 0.5 collective-permute-start.11
  113.7 1.7 %collective-permute-start.12 = (f32[1,32,1152]{2,1,0:T(8,128)S(1)}, f32[1,32,1152]{2,1,0:T(8,128)S(1)}, u32[]{:S(2)}, u32[]{:S(2)}) collective-permute-start(f32[1,32,1152]{2,1,0:T(8,128)S(1)} %get-tuple-element.12), channel_id=1, source_target_pairs={{0,2},{1,3},{2,4},{3,5},{4,6},{5,7},{6,0},{7,1},{8,10},{9,11},{10,... | collective-permute-start | bytes 442376 | tf_op jit(solution)/shard_map/ppermute | solution.py:101
  115.4 0.8 collective-permute-start.13
  116.2 1.2 collective-permute-start.14
  117.4 0.7 collective-permute-start.15
  118.1 6.7 %collective-permute-done.11 = f32[1,32,1152]{2,1,0:T(8,128)S(1)} collective-permute-done((f32[1,32,1152]{2,1,0:T(8,128)S(1)}, f32[1,32,1152]{2,1,0:T(8,128)S(1)}, u32[]{:S(2)}, u32[]{:S(2)}) %collective-permute-start.11) | collective-permute-done | bytes 147488 | tf_op jit(solution)/shard_map/ppermute | solution.py:101
  124.9 19.1 %all_to_all.24 = f32[128,8,1]{1,2,0:T(1,128)S(1)} all-to-all(f32[128,8,1]{1,2,0:T(1,128)S(1)} %bitcast.72), channel_id=1, replica_groups=mesh['z'=4,'core'=2,'yhi'=2,'ylo'=2,'x'=4] {'z','yhi','core','ylo','x'}, dimensions={0} | all-to-all | bytes 8192 | tf_op jit(solution)/shard_map/all_to_all | solution.py:87
  144.0 0.5 broadcast.141
  144.5 0.8 reduce.11
  145.7 3.2 %collective-permute-start.18 = (f32[32,1024]{1,0:T(8,128)S(1)}, f32[32,1024]{1,0:T(8,128)S(1)}, u32[]{:S(2)}, u32[]{:S(2)}) collective-permute-start(f32[32,1024]{1,0:T(8,128)S(1)} %fusion.33), channel_id=1, source_target_pairs={{0,0},{8,16},{16,8},{24,24},{1,1},{9,17},{17,9},{25,25},{2,2},{10,... | collective-permute-start | bytes 393224 | tf_op jit(solution)/shard_map/ppermute | solution.py:142
  149.0 0.9 select_reduce_fusion
  149.9 3.7 %collective-permute-done.18 = f32[32,1024]{1,0:T(8,128)S(1)} collective-permute-done((f32[32,1024]{1,0:T(8,128)S(1)}, f32[32,1024]{1,0:T(8,128)S(1)}, u32[]{:S(2)}, u32[]{:S(2)}) %collective-permute-start.18) | collective-permute-done | bytes 131104 | tf_op jit(solution)/shard_map/ppermute | solution.py:142
  153.5 0.7 copy.34
  (64 shorter events, 4.7 us)
Async XLA Ops:
  0.6 3.1 %copy-start.3 = (bf16[512,1024]{1,0:T(8,128)(2,1)S(1)}, bf16[512,1024]{1,0:T(8,128)(2,1)}, u32[]{:S(2)}) copy-start(bf16[512,1024]{1,0:T(8,128)(2,1)} %param.3) | copy-start | bytes 3145732
  6.8 11.5 %copy-start.4 = (bf16[512,1024]{1,0:T(8,128)(2,1)S(1)}, bf16[512,1024]{1,0:T(8,128)(2,1)}, u32[]{:S(2)}) copy-start(bf16[512,1024]{1,0:T(8,128)(2,1)} %param.5) | copy-start | bytes 3145732
  6.8 41.8 %all-to-all-start = ((bf16[128,8,1024]{2,1,0:T(8,128)(2,1)}), bf16[128,8,1024]{2,1,0:T(8,128)(2,1)S(1)}, u32[]{:S(2)}, u32[]{:S(2)}) async-start(bf16[128,8,1024]{2,1,0:T(8,128)(2,1)} %select_bitcast_fusion), calls=%async_computation | async-start | bytes 4194304 | tf_op jit(solution)/shard_map/all_to_all | solution.py:62
  18.3 3.6 %collective-permute-start = (bf16[512,1024]{1,0:T(8,128)(2,1)S(1)}, bf16[512,1024]{1,0:T(8,128)(2,1)}, u32[]{:S(2)}, u32[]{:S(2)}) collective-permute-start(bf16[512,1024]{1,0:T(8,128)(2,1)S(1)} %copy-done.4), channel_id=1, source_target_pairs={{0,16},{16,0},{1,17},{17,1},{2,18},{18,2},{3,19},{19,3},{4,20},{20... | collective-permute-start | bytes 3145736 | tf_op jit(solution)/shard_map/ppermute | solution.py:37
  50.1 1.3 copy-start.2
  59.2 1.4 copy-start.1
  60.6 3.9 %collective-permute-start.1 = (f32[8,32,1152]{2,1,0:T(8,128)S(1)}, f32[8,32,1152]{2,1,0:T(8,128)}, u32[]{:S(2)}, u32[]{:S(2)}) collective-permute-start(f32[8,32,1152]{2,1,0:T(8,128)S(1)} %dynamic-slice_bitcast_fusion.1), channel_id=1, source_target_pairs={{0,16},{16,0},{1,17},{17,1},{2,18},{18,2},{3,19},{19,3},{4,20},{20... | collective-permute-start | bytes 3538952 | tf_op jit(solution)/shard_map/ppermute | solution.py:97
  67.3 11.9 %collective-permute-start.2 = (f32[1,32,1152]{2,1,0:T(8,128)S(1)}, f32[1,32,1152]{2,1,0:T(8,128)S(1)}, u32[]{:S(2)}, u32[]{:S(2)}) collective-permute-start(f32[1,32,1152]{2,1,0:T(8,128)S(1)} %get-tuple-element.15), channel_id=1, source_target_pairs={{0,1},{1,2},{2,3},{3,4},{4,5},{5,6},{6,7},{7,0},{8,9},{9,10},{10,1... | collective-permute-start | bytes 442376 | tf_op jit(solution)/shard_map/ppermute | solution.py:101
  67.6 11.7 %collective-permute-start.3 = (f32[1,32,1152]{2,1,0:T(8,128)S(1)}, f32[1,32,1152]{2,1,0:T(8,128)}, u32[]{:S(2)}, u32[]{:S(2)}) collective-permute-start(f32[1,32,1152]{2,1,0:T(8,128)S(1)} %get-tuple-element.21), channel_id=1, source_target_pairs={{0,2},{1,3},{2,4},{3,5},{4,6},{5,7},{6,0},{7,1},{8,10},{9,11},{10,... | collective-permute-start | bytes 442376 | tf_op jit(solution)/shard_map/ppermute | solution.py:101
  68.9 11.3 %collective-permute-start.4 = (f32[1,32,1152]{2,1,0:T(8,128)}, f32[1,32,1152]{2,1,0:T(8,128)}, u32[]{:S(2)}, u32[]{:S(2)}) collective-permute-start(f32[1,32,1152]{2,1,0:T(8,128)} %get-tuple-element.20), channel_id=1, source_target_pairs={{0,3},{1,4},{2,5},{3,6},{4,7},{5,0},{6,1},{7,2},{8,11},{9,12},{10,... | collective-permute-start | bytes 442376 | tf_op jit(solution)/shard_map/ppermute | solution.py:101
  69.5 15.3 %collective-permute-start.5 = (f32[1,32,1152]{2,1,0:T(8,128)}, f32[1,32,1152]{2,1,0:T(8,128)}, u32[]{:S(2)}, u32[]{:S(2)}) collective-permute-start(f32[1,32,1152]{2,1,0:T(8,128)} %get-tuple-element.19), channel_id=1, source_target_pairs={{0,4},{1,5},{2,6},{3,7},{4,0},{5,1},{6,2},{7,3},{8,12},{9,13},{10,... | collective-permute-start | bytes 442376 | tf_op jit(solution)/shard_map/ppermute | solution.py:101
  71.1 13.6 %collective-permute-start.6 = (f32[1,32,1152]{2,1,0:T(8,128)}, f32[1,32,1152]{2,1,0:T(8,128)}, u32[]{:S(2)}, u32[]{:S(2)}) collective-permute-start(f32[1,32,1152]{2,1,0:T(8,128)} %get-tuple-element.18), channel_id=1, source_target_pairs={{0,5},{1,6},{2,7},{3,0},{4,1},{5,2},{6,3},{7,4},{8,13},{9,14},{10,... | collective-permute-start | bytes 442376 | tf_op jit(solution)/shard_map/ppermute | solution.py:101
  79.2 5.8 %collective-permute-start.7 = (f32[1,32,1152]{2,1,0:T(8,128)}, f32[1,32,1152]{2,1,0:T(8,128)}, u32[]{:S(2)}, u32[]{:S(2)}) collective-permute-start(f32[1,32,1152]{2,1,0:T(8,128)} %get-tuple-element.17), channel_id=1, source_target_pairs={{0,6},{1,7},{2,0},{3,1},{4,2},{5,3},{6,4},{7,5},{8,14},{9,15},{10,... | collective-permute-start | bytes 442376 | tf_op jit(solution)/shard_map/ppermute | solution.py:101
  79.2 6.1 %collective-permute-start.8 = (f32[1,32,1152]{2,1,0:T(8,128)}, f32[1,32,1152]{2,1,0:T(8,128)}, u32[]{:S(2)}, u32[]{:S(2)}) collective-permute-start(f32[1,32,1152]{2,1,0:T(8,128)} %get-tuple-element.16), channel_id=1, source_target_pairs={{0,7},{1,0},{2,1},{3,2},{4,3},{5,4},{6,5},{7,6},{8,15},{9,8},{10,9... | collective-permute-start | bytes 442376 | tf_op jit(solution)/shard_map/ppermute | solution.py:101
  100.3 5.4 %collective-permute-start.9 = (bf16[8,32,1152]{2,1,0:T(8,128)(2,1)S(1)}, bf16[8,32,1152]{2,1,0:T(8,128)(2,1)S(1)}, u32[]{:S(2)}, u32[]{:S(2)}) collective-permute-start(bf16[8,32,1152]{2,1,0:T(8,128)(2,1)S(1)} %all_to_all.23), channel_id=1, source_target_pairs={{0,16},{16,0},{1,17},{17,1},{2,18},{18,2},{3,19},{19,3},{4,20},{20... | collective-permute-start | bytes 1769480 | tf_op jit(solution)/shard_map/ppermute | solution.py:129
  106.2 1.8 %copy-start = (bf16[1024,1152]{1,0:T(8,128)(2,1)S(1)}, bf16[1024,1152]{1,0:T(8,128)(2,1)}, u32[]{:S(2)}) copy-start(bf16[1024,1152]{1,0:T(8,128)(2,1)} %concatenate.10) | copy-start | bytes 7077892
  110.0 2.9 %collective-permute-start.10 = (f32[8,32,1152]{2,1,0:T(8,128)S(1)}, f32[8,32,1152]{2,1,0:T(8,128)S(1)}, u32[]{:S(2)}, u32[]{:S(2)}) collective-permute-start(f32[8,32,1152]{2,1,0:T(8,128)S(1)} %dynamic-slice_bitcast_fusion), channel_id=1, source_target_pairs={{0,16},{16,0},{1,17},{17,1},{2,18},{18,2},{3,19},{19,3},{4,20},{20... | collective-permute-start | bytes 3538952 | tf_op jit(solution)/shard_map/ppermute | solution.py:97
  113.2 11.6 %collective-permute-start.11 = (f32[1,32,1152]{2,1,0:T(8,128)S(1)}, f32[1,32,1152]{2,1,0:T(8,128)S(1)}, u32[]{:S(2)}, u32[]{:S(2)}) collective-permute-start(f32[1,32,1152]{2,1,0:T(8,128)S(1)} %get-tuple-element.6), channel_id=1, source_target_pairs={{0,1},{1,2},{2,3},{3,4},{4,5},{5,6},{6,7},{7,0},{8,9},{9,10},{10,1... | collective-permute-start | bytes 442376 | tf_op jit(solution)/shard_map/ppermute | solution.py:101
  113.7 11.1 %collective-permute-start.12 = (f32[1,32,1152]{2,1,0:T(8,128)S(1)}, f32[1,32,1152]{2,1,0:T(8,128)S(1)}, u32[]{:S(2)}, u32[]{:S(2)}) collective-permute-start(f32[1,32,1152]{2,1,0:T(8,128)S(1)} %get-tuple-element.12), channel_id=1, source_target_pairs={{0,2},{1,3},{2,4},{3,5},{4,6},{5,7},{6,0},{7,1},{8,10},{9,11},{10,... | collective-permute-start | bytes 442376 | tf_op jit(solution)/shard_map/ppermute | solution.py:101
  115.4 30.0 %collective-permute-start.13 = (f32[1,32,1152]{2,1,0:T(8,128)S(1)}, f32[1,32,1152]{2,1,0:T(8,128)S(1)}, u32[]{:S(2)}, u32[]{:S(2)}) collective-permute-start(f32[1,32,1152]{2,1,0:T(8,128)S(1)} %get-tuple-element.11), channel_id=1, source_target_pairs={{0,3},{1,4},{2,5},{3,6},{4,7},{5,0},{6,1},{7,2},{8,11},{9,12},{10,... | collective-permute-start | bytes 442376 | tf_op jit(solution)/shard_map/ppermute | solution.py:101
  116.2 29.2 %collective-permute-start.14 = (f32[1,32,1152]{2,1,0:T(8,128)S(1)}, f32[1,32,1152]{2,1,0:T(8,128)S(1)}, u32[]{:S(2)}, u32[]{:S(2)}) collective-permute-start(f32[1,32,1152]{2,1,0:T(8,128)S(1)} %get-tuple-element.10), channel_id=1, source_target_pairs={{0,4},{1,5},{2,6},{3,7},{4,0},{5,1},{6,2},{7,3},{8,12},{9,13},{10,... | collective-permute-start | bytes 442376 | tf_op jit(solution)/shard_map/ppermute | solution.py:101
  117.4 28.0 %collective-permute-start.15 = (f32[1,32,1152]{2,1,0:T(8,128)S(1)}, f32[1,32,1152]{2,1,0:T(8,128)S(1)}, u32[]{:S(2)}, u32[]{:S(2)}) collective-permute-start(f32[1,32,1152]{2,1,0:T(8,128)S(1)} %get-tuple-element.9), channel_id=1, source_target_pairs={{0,5},{1,6},{2,7},{3,0},{4,1},{5,2},{6,3},{7,4},{8,13},{9,14},{10,... | collective-permute-start | bytes 442376 | tf_op jit(solution)/shard_map/ppermute | solution.py:101
  124.8 20.6 %collective-permute-start.16 = (f32[1,32,1152]{2,1,0:T(8,128)S(1)}, f32[1,32,1152]{2,1,0:T(8,128)S(1)}, u32[]{:S(2)}, u32[]{:S(2)}) collective-permute-start(f32[1,32,1152]{2,1,0:T(8,128)S(1)} %get-tuple-element.8), channel_id=1, source_target_pairs={{0,6},{1,7},{2,0},{3,1},{4,2},{5,3},{6,4},{7,5},{8,14},{9,15},{10,... | collective-permute-start | bytes 442376 | tf_op jit(solution)/shard_map/ppermute | solution.py:101
  124.8 20.7 %collective-permute-start.17 = (f32[1,32,1152]{2,1,0:T(8,128)S(1)}, f32[1,32,1152]{2,1,0:T(8,128)S(1)}, u32[]{:S(2)}, u32[]{:S(2)}) collective-permute-start(f32[1,32,1152]{2,1,0:T(8,128)S(1)} %get-tuple-element.7), channel_id=1, source_target_pairs={{0,7},{1,0},{2,1},{3,2},{4,3},{5,4},{6,5},{7,6},{8,15},{9,8},{10,9... | collective-permute-start | bytes 442376 | tf_op jit(solution)/shard_map/ppermute | solution.py:101
  145.7 7.8 %collective-permute-start.18 = (f32[32,1024]{1,0:T(8,128)S(1)}, f32[32,1024]{1,0:T(8,128)S(1)}, u32[]{:S(2)}, u32[]{:S(2)}) collective-permute-start(f32[32,1024]{1,0:T(8,128)S(1)} %fusion.33), channel_id=1, source_target_pairs={{0,0},{8,16},{16,8},{24,24},{1,1},{9,17},{17,9},{25,25},{2,2},{10,... | collective-permute-start | bytes 393224 | tf_op jit(solution)/shard_map/ppermute | solution.py:142
